TPU v7x, 32 devices: a whole 2x2x4 slice. The times are simulated.
32 devices in a mesh: gx: 4 (over z), gy: 8 (over y, x, core).
Axes of the slice: x: 2, y: 2, z: 4, core: 2. Of those that a mesh axis runs over, the one named last changes fastest.
Arguments:
- adjoint: float32 [3, 66, 131072], P(None, None, ('gx', 'gy')), may hold values from -6 to 6
- deriv_r: float32 [66, 66], replicated, may hold values from -0.75 to 0.75
- deriv_s: float32 [66, 66], replicated, may hold values from -0.75 to 0.75
- lift: float32 [66, 33], replicated, may hold values from -0.75 to 0.75
- metric: float32 [4, 131072], P(None, ('gx', 'gy')), may hold values from -1.5 to 1.5
- face_scale: float32 [3, 131072], P(None, ('gx', 'gy')), may hold values from 0.5 to 4
- face_angle: float32 [3, 131072], P(None, ('gx', 'gy')), may hold values from -3.140625 to 3.140625
- neighbours: int32 [3, 131072], P(None, ('gx', 'gy')), may hold values from 0 to 131071, as said below
- neighbour_face: int32 [3, 131072], P(None, ('gx', 'gy')), may hold values from 0 to 2, as said below
- remap_table: float32 [16, 66, 66], replicated, may hold values from -0.75 to 0.75
- intersection_elem: int32 [262144], P(('gx', 'gy')), may hold values from 0 to 4095
- intersection_old: int32 [262144], P(('gx', 'gy')), may hold values from -1 to 2047, as said below
- intersection_weight: float32 [262144], P(('gx', 'gy')), may hold values from 0.05 to 1
- block_type: int32 [2048], P(('gx', 'gy')), may hold values from 0 to 15
Outputs:
- adj_new: float32 [3, 66, 131072], P(None, None, ('gx', 'gy'))
- adj_old: float32 [3, 66, 65536], P(None, None, ('gx', 'gy'))
Inputs may be any that keep to these rules, and one draw needn't show every extreme that they name: `neighbours`: the face relation is symmetric: the element across face g of e has e across face neighbour_face[g, e]; the element across lies fewer than 32 positions from e in the slab's element order, counted cyclically. `neighbour_face`: faces are numbered 0, 1, 2. `intersection_old`: -1 marks a padded row; in every draw some devices have all their rows live, and some owner receives full groups from every device within 4 of it. `intersection_elem`: index of the new element on the device that holds the row.
All inputs are finite; a program needn't handle non-finite values.
Results may differ from a plain program's by a relative error of at most 0.00007.
Values sent between devices are 32-bit elements; how exact they have to be, the bound alone decides.
No kernel may reach another device: no remote copies, remote signals or barrier semaphores. Data moves between devices by JAX's collectives and lax.ppermute only.
A program may use at most 192 MiB of HBM per device.

v0:
```python
import jax
import jax.numpy as jnp
import numpy as np
from jax import lax
from jax.sharding import PartitionSpec as P

ORDER = 10
E_OLD_DEV = 2048
REACH = 4
BLOCK = 128
RIM = 32


gravity = 2.0
depth = 0.5
wave_speed = 1.0
time_step = 0.04
highest = lax.Precision.HIGHEST


def extended(cells, sides, width):
    for axis, dim in sides:
        count = lax.axis_size(axis)
        head = lax.slice_in_dim(cells, 0, width, axis=dim)
        tail = lax.slice_in_dim(cells, cells.shape[dim] - width, cells.shape[dim], axis=dim)
        cells = jnp.concatenate(
            [
                lax.ppermute(tail, axis, [(i, (i + 1) % count) for i in range(count)]),
                cells,
                lax.ppermute(head, axis, [((i + 1) % count, i) for i in range(count)]),
            ],
            axis=dim,
        )
    return cells


def shifted(shard, axis, by):
    length = lax.axis_size(axis)
    return lax.ppermute(shard, axis, [(i, (i + by) % length) for i in range(length)])


def face_table(degree):
    basis_count = (degree + 1) * (degree + 2) // 2

    def node_place(column, level):
        return level * (degree + 1) - level * (level - 1) // 2 + column

    ones_table = np.zeros((3, degree + 1, basis_count), np.float32)
    for level in range(degree + 1):
        ones_table[0, level, node_place(level, 0)] = 1.0
        ones_table[1, level, node_place(degree - level, level)] = 1.0
        ones_table[2, level, node_place(0, degree - level)] = 1.0
    return jnp.asarray(ones_table)


def group_bounds(q_rows, reach):
    cap_far = q_rows // 32
    cap_near = q_rows // 8
    cap_home = q_rows - 2 * cap_near - 2 * (reach - 1) * cap_far
    bounds = []
    start = 0
    for offset in range(-reach, reach + 1):
        if offset == 0:
            group_size = cap_home
        elif abs(offset) == 1:
            group_size = cap_near
        else:
            group_size = cap_far
        bounds.append((offset, start, group_size))
        start = start + group_size
    return bounds


def volume_terms(current, deriv_r, deriv_s, metric):
    along_r = jnp.einsum("pq,fpe->fqe", deriv_r, current, precision=highest)
    along_s = jnp.einsum("pq,fpe->fqe", deriv_s, current, precision=highest)
    to_height = -gravity * (
        metric[0] * along_r[1]
        + metric[1] * along_s[1]
        + metric[2] * along_r[2]
        + metric[3] * along_s[2]
    )
    to_along_x = -depth * (metric[0] * along_r[0] + metric[1] * along_s[0])
    to_along_y = -depth * (metric[2] * along_r[0] + metric[3] * along_s[0])
    return jnp.stack([to_height, to_along_x, to_along_y])


def face_terms(current, lift, face_scale, face_angle):
    lift_faces = lift.reshape(lift.shape[0], 3, -1)
    lifted = jnp.einsum("pgn,fpe->fnge", lift_faces, current, precision=highest)
    normal_x = jnp.cos(face_angle)[None]
    normal_y = jnp.sin(face_angle)[None]
    half_scale = 0.5 * face_scale[None]
    height, along_x, along_y = (lifted[0], lifted[1], lifted[2])
    face_height = half_scale * (
        gravity * (normal_x * along_x + normal_y * along_y) - wave_speed * height
    )
    face_along_x = half_scale * (depth * normal_x * height - wave_speed * along_x)
    face_along_y = half_scale * (depth * normal_y * height - wave_speed * along_y)
    return jnp.stack([face_height, face_along_x, face_along_y])


def body(
    adjoint,
    deriv_r,
    deriv_s,
    lift,
    metric,
    face_scale,
    face_angle,
    neighbours,
    neighbour_face,
    remap_table,
    intersection_elem,
    intersection_old,
    intersection_weight,
    block_type,
):
    face_ones = face_table(ORDER)
    elem_count = adjoint.shape[2]
    basis_count = adjoint.shape[1]
    devices = lax.axis_size(("gx", "gy"))
    elem_total = elem_count * devices
    first_elem = lax.axis_index(("gx", "gy")) * elem_count
    local_index = (neighbours - first_elem + RIM + elem_total) % elem_total
    flat_index = neighbour_face * (elem_count + 2 * RIM) + local_index

    def advance(current):
        volume = volume_terms(current, deriv_r, deriv_s, metric)
        traces = face_terms(current, lift, face_scale, face_angle)
        traces_wide = extended(traces, ((("gx", "gy"), 3),), RIM)
        flattened = traces_wide.reshape(3, traces_wide.shape[1], -1)
        outside = jnp.take(flattened, flat_index, axis=2)
        jump_terms = traces - outside[:, ::-1]
        surface = jnp.einsum("gnp,fnge->fpe", face_ones, jump_terms, precision=highest)
        return current + time_step * (volume + surface)

    section_two = 2.0 / 3.0 * advance(adjoint)
    section_one = 0.25 * advance(section_two)
    adj_new = adjoint / 3.0 + 0.75 * section_two + advance(section_one)
    rows_here = intersection_elem.shape[0]
    block_here = rows_here // BLOCK
    field_rows = 3 * basis_count
    picked = jnp.take(adj_new, intersection_elem, axis=2)
    picked = picked.reshape(3, basis_count, block_here, BLOCK)
    chosen = jnp.take(remap_table, block_type, axis=0)
    mapped = jnp.einsum("bij,fibr->fjbr", chosen, picked, precision=highest)
    mapped = (mapped * intersection_weight.reshape(1, 1, block_here, BLOCK)).reshape(
        3, basis_count, rows_here
    )
    bounds = group_bounds(rows_here, REACH)
    kept_values = []
    kept_labels = []
    for offset, start, group_size in bounds:
        if offset == 0:
            kept_values.append(mapped[:, :, start : start + group_size])
            kept_labels.append(intersection_old[start : start + group_size])
    for offset, start, group_size in bounds:
        if offset != 0:
            piece = mapped[:, :, start : start + group_size]
            piece_labels = intersection_old[start : start + group_size]
            got_values, got_labels = shifted((piece, piece_labels), ("gx", "gy"), offset)
            kept_values.append(got_values)
            kept_labels.append(got_labels)
    received = jnp.concatenate(kept_values, axis=2).reshape(field_rows, -1)
    received_labels = jnp.concatenate(kept_labels, axis=0)
    old_iota = jnp.arange(E_OLD_DEV, dtype=jnp.int32)[None, :]
    selector = (received_labels[:, None] == old_iota).astype(jnp.float32)
    old_sums = jnp.dot(received, selector, precision=highest, preferred_element_type=jnp.float32)
    return (adj_new, old_sums.reshape(3, basis_count, E_OLD_DEV))


def solution(mesh):
    in_specs = (
        P(None, None, ("gx", "gy")),
        P(),
        P(),
        P(),
        P(None, ("gx", "gy")),
        P(None, ("gx", "gy")),
        P(None, ("gx", "gy")),
        P(None, ("gx", "gy")),
        P(None, ("gx", "gy")),
        P(),
        P(("gx", "gy")),
        P(("gx", "gy")),
        P(("gx", "gy")),
        P(("gx", "gy")),
    )
    out_specs = (P(None, None, ("gx", "gy")), P(None, None, ("gx", "gy")))
    return jax.shard_map(body, mesh=mesh, in_specs=in_specs, out_specs=out_specs, check_vma=False)
```

profile of v0, /device:TPU:0, one launch (start us, length us, event | category | flops | bytes accessed | tf_op | source)
XLA Modules:
  0.0 803.9 jit_solution(5225547834339105724)
XLA Ops:
  3.7 4.9 convolution_bitcast_fusion.11
  11.1 6.0 collective-permute-start.1
  25.7 7.4 convolution_bitcast_fusion.7
  33.1 5.3 convolution_bitcast_fusion.8
  38.4 5.9 gather_fusion.1
  44.3 3.6 select_bitcast_fusion.3
  47.9 4.3 fusion.43
  63.2 4.3 collective-permute-done.21
  67.6 2.5 concatenate.15
  70.1 18.7 %copy.62 = f32[3,11,3,4160]{1,0,3,2:T(4,128)} copy(f32[3,11,3,4160]{3,1,2,0:T(8,128)} %concatenate.15) | data formatting | bytes 3294720 | tf_op jit(solution)/shard_map/reshape | solution.py:132
  88.8 97.2 %gather_fusion.2 = f32[12288,3,11]{2,1,0:T(4,128)} fusion(f32[3,11,12480]{1,0,2:T(4,128)} %bitcast.135, s32[12288]{0:T(1024)S(1)} %broadcast_clamp_fusion), kind=kCustom, calls=%fused_computation.clone | custom fusion | bytes 3293184 | tf_op jit(solution)/shard_map/jit(_take)/gather | solution.py:133
  186.0 19.4 %copy.30 = f32[3,4096,3,11]{1,3,0,2:T(8,128)} copy(f32[3,4096,3,11]{3,2,1,0:T(4,128)} %bitcast.138) | data formatting | bytes 3244032 | tf_op jit(solution)/shard_map/jit(_take)/gather | solution.py:133
  207.3 11.0 %rev.9 = f32[3,11,3,4096]{3,1,2,0:T(8,128)} reverse(f32[3,11,3,4096]{3,1,2,0:T(8,128)S(1)} %select_bitcast_fusion.2), dimensions={1} | reverse | bytes 3244032 | tf_op jit(solution)/shard_map/rev | solution.py:134
  218.3 8.5 %fusion.8 = f32[3,66,4096]{2,1,0:T(8,128)S(1)} fusion(f32[3,66,4096]{2,1,0:T(8,128)} %param.17, f32[3,11,66,1]{2,1,0,3:T(8,128)} %constant.93, f32[1,66,4096]{2,1,0:T(8,128)} %get-tuple-element.12, f32[1,66,4096]{2,1,0:T(8,128)} %get-tuple-element.13, f32[1,66,4096]{2,1,0:T(8,128)} %get-tuple-element.11, f32[3,11,3,4096]{3,1,2,0:T(8,128)} %rev.9, ...), kind=kOutput, calls=%fused_computation.23 | convolution fusion | flops 326430720 | bytes 12984840 | tf_op jit(solution)/shard_map/gnp,fnge->fpe/dot_general | solution.py:135
  226.8 3.1 convolution_bitcast_fusion.10
  230.0 3.9 convolution_bitcast_fusion.4
  233.9 4.1 convolution_bitcast_fusion.5
  241.3 5.3 collective-permute-start.3
  249.6 4.3 concatenate.16
  253.9 18.7 %copy.67 = f32[3,11,3,4160]{1,0,3,2:T(4,128)} copy(f32[3,11,3,4160]{3,1,2,0:T(8,128)} %concatenate.16) | data formatting | bytes 3294720 | tf_op jit(solution)/shard_map/reshape | solution.py:132
  272.6 97.3 %gather_fusion.3 = f32[12288,3,11]{2,1,0:T(4,128)} fusion(f32[3,11,12480]{1,0,2:T(4,128)} %bitcast.136, s32[12288]{0:T(1024)} %copy-done.23), kind=kCustom, calls=%fused_computation.1.clone | custom fusion | bytes 3293184 | tf_op jit(solution)/shard_map/jit(_take)/gather | solution.py:133
  369.9 19.4 %copy.36 = f32[3,4096,3,11]{1,3,0,2:T(8,128)} copy(f32[3,4096,3,11]{3,2,1,0:T(4,128)} %bitcast.139) | data formatting | bytes 3244032 | tf_op jit(solution)/shard_map/jit(_take)/gather | solution.py:133
  389.3 3.4 select_bitcast_fusion.1
  392.6 17.4 %rev.10 = f32[3,11,3,4096]{3,1,2,0:T(8,128)} reverse(f32[3,11,3,4096]{3,1,2,0:T(8,128)} %select_bitcast_fusion.1), dimensions={1} | reverse | bytes 3244032 | tf_op jit(solution)/shard_map/rev | solution.py:134
  410.0 7.6 fusion.12
  417.7 2.9 convolution_bitcast_fusion.9
  420.6 3.4 convolution_bitcast_fusion.1
  424.1 3.7 convolution_bitcast_fusion.2
  431.1 5.3 collective-permute-start.5
  439.4 4.3 concatenate.17
  443.7 18.7 %copy.72 = f32[3,11,3,4160]{1,0,3,2:T(4,128)} copy(f32[3,11,3,4160]{3,1,2,0:T(8,128)} %concatenate.17) | data formatting | bytes 3294720 | tf_op jit(solution)/shard_map/reshape | solution.py:132
  462.4 97.3 %gather_fusion.4 = f32[12288,3,11]{2,1,0:T(4,128)} fusion(f32[3,11,12480]{1,0,2:T(4,128)} %bitcast.134, s32[12288]{0:T(1024)} %copy-done.23), kind=kCustom, calls=%fused_computation.2.clone | custom fusion | bytes 3293184 | tf_op jit(solution)/shard_map/jit(_take)/gather | solution.py:133
  559.7 19.4 %copy.42 = f32[3,4096,3,11]{1,3,0,2:T(8,128)} copy(f32[3,4096,3,11]{3,2,1,0:T(4,128)} %bitcast.137) | data formatting | bytes 3244032 | tf_op jit(solution)/shard_map/jit(_take)/gather | solution.py:133
  579.1 3.4 select_bitcast_fusion
  582.4 17.4 %rev.11 = f32[3,11,3,4096]{3,1,2,0:T(8,128)} reverse(f32[3,11,3,4096]{3,1,2,0:T(8,128)} %select_bitcast_fusion), dimensions={1} | reverse | bytes 3244032 | tf_op jit(solution)/shard_map/rev | solution.py:134
  599.8 11.8 %fusion.16 = f32[3,66,4096]{2,1,0:T(8,128)} fusion(f32[3,66,4096]{2,1,0:T(8,128)} %copy-done.3, f32[3,11,66,1]{2,1,0,3:T(8,128)} %constant.93, f32[1,66,4096]{2,1,0:T(8,128)} %get-tuple-element.6, f32[1,66,4096]{2,1,0:T(8,128)} %get-tuple-element.7, f32[1,66,4096]{2,1,0:T(8,128)} %get-tuple-element.5, f32[3,66,4096]{2,1,0:T(8,128)S(1)} %fusion.8, ...), kind=kOutput, calls=%fused_computation.31 | convolution fusion | flops 329674752 | bytes 19472904 | tf_op jit(solution)/shard_map/gnp,fnge->fpe/dot_general | solution.py:135
  611.6 8.3 %copy.43 = f32[3,66,4096]{1,0,2:T(4,128)} copy(f32[3,66,4096]{2,1,0:T(8,128)} %fusion.16) | data formatting | bytes 6488064 | tf_op jit(solution)/shard_map/add | solution.py:140
  619.9 63.1 %gather_fusion = f32[8192,3,66]{2,1,0:T(4,128)} fusion(f32[3,66,4096]{1,0,2:T(4,128)} %copy.43, s32[8192]{0:T(1024)S(1)} %copy-done.54), kind=kCustom, calls=%fused_computation.3 | custom fusion | bytes 13008896 | tf_op jit(solution)/shard_map/jit(_take)/gather | solution.py:144
  682.9 15.4 %copy.44 = f32[3,66,64,128]{3,1,0,2:T(8,128)} copy(f32[3,66,64,128]{1,0,3,2:T(4,128)} %bitcast.133) | data formatting | bytes 12976128 | tf_op jit(solution)/shard_map/jit(_take)/gather | solution.py:144
  698.4 12.6 %multiply_bitcast_fusion = f32[3,66,64,128]{3,1,0,2:T(8,128)S(1)} fusion(f32[64,128]{1,0:T(8,128)S(1)} %bitcast.152, f32[3,66,64,128]{3,1,0,2:T(8,128)} %copy.44, pred[64,128]{1,0:T(8,128)(4,1)S(1)} %copy-done.61, f32[64,66,66,1]{2,0,1,3:T(8,128)S(1)} %copy-done.7), kind=kOutput, calls=%fused_computation.9 | convolution fusion | flops 1287880704 | bytes 14132224 | tf_op jit(solution)/shard_map/bij,fibr->fjbr/dot_general | solution.py:147
  711.0 3.9 copy.46
  714.9 7.3 reshape.203
  725.4 4.6 collective-permute-start.9
  730.1 2.4 slice_dynamic-update-slice_fusion
  737.8 17.9 %collective-permute-done.8 = f32[3,66,256]{2,1,0:T(8,128)S(1)} collective-permute-done((f32[3,66,256]{2,1,0:T(8,128)S(1)}, f32[3,66,256]{2,1,0:T(8,128)S(1)}, u32[]{:S(2)}, u32[]{:S(2)}) %collective-permute-start.8) | collective-permute-done | bytes 202784 | tf_op jit(solution)/shard_map/ppermute | solution.py:39
  755.7 8.8 %collective-permute-start.13 = (f32[3,66,256]{2,1,0:T(8,128)S(1)}, f32[3,66,256]{2,1,0:T(8,128)S(1)}, u32[]{:S(2)}, u32[]{:S(2)}) collective-permute-start(f32[3,66,256]{2,1,0:T(8,128)S(1)} %get-tuple-element.14), channel_id=1, source_target_pairs={{0,4},{1,5},{2,6},{3,7},{4,8},{5,9},{6,10},{7,11},{8,12},{9,13},{1... | collective-permute-start | bytes 608264 | tf_op jit(solution)/shard_map/ppermute | solution.py:39
  764.9 3.5 collective-permute-done.13
  768.4 35.1 %fusion.1 = f32[3,66,2048]{2,1,0:T(8,128)} fusion(f32[3,66,8192]{2,1,0:T(8,128)S(1)} %constant_dynamic-update-slice_fusion, s32[8192]{0:T(1024)S(1)} %copy-done.67), kind=kOutput, calls=%fused_computation.7 | convolution fusion | flops 39879442432 | bytes 8142848 | tf_op jit(solution)/shard_map/dot_general | solution.py:169
  (221 shorter events, 47.8 us)
Async XLA Ops:
  0.6 37.8 %copy-start = (f32[16,66,66]{2,0,1:T(8,128)S(1)}, f32[16,66,66]{2,0,1:T(8,128)}, u32[]{:S(2)}) copy-start(f32[16,66,66]{2,0,1:T(8,128)} %param.26) | copy-start | bytes 836356
  9.1 12.9 %copy-start.68 = (s32[64]{0:T(128)S(1)}, s32[64]{0:T(128)}, u32[]{:S(2)}) copy-start(s32[64]{0:T(128)} %param.30) | copy-start | bytes 772
  9.2 14.0 %copy-start.55 = (s32[8192]{0:T(1024)S(1)}, s32[8192]{0:T(1024)}, u32[]{:S(2)}) copy-start(s32[8192]{0:T(1024)} %param.27) | copy-start | bytes 98308
  9.2 15.2 %copy-start.58 = (s32[3,4096]{1,0:T(4,128)S(1)}, s32[3,4096]{1,0:T(4,128)}, u32[]{:S(2)}) copy-start(s32[3,4096]{1,0:T(4,128)} %param.24) | copy-start | bytes 147460
  9.2 15.2 %copy-start.59 = (s32[3,4096]{1,0:T(4,128)S(1)}, s32[3,4096]{1,0:T(4,128)}, u32[]{:S(2)}) copy-start(s32[3,4096]{1,0:T(4,128)} %param.25) | copy-start | bytes 147460
  9.2 16.4 %copy-start.36 = (f32[66,66]{1,0:T(8,128)S(1)}, f32[66,66]{1,0:T(8,128)}, u32[]{:S(2)}) copy-start(f32[66,66]{1,0:T(8,128)} %param.19) | copy-start | bytes 52276
  10.6 57.0 %collective-permute-start = (f32[3,11,3,32]{3,1,2,0:T(8,128)S(1)}, f32[3,11,3,32]{3,1,2,0:T(8,128)S(1)}, u32[]{:S(2)}, u32[]{:S(2)}) collective-permute-start(f32[3,11,3,32]{3,1,2,0:T(8,128)S(1)} %get-tuple-element.36), channel_id=1, source_target_pairs={{0,1},{1,2},{2,3},{3,4},{4,5},{5,6},{6,7},{7,8},{8,9},{9,10},{10,1... | collective-permute-start | bytes 38024 | tf_op jit(solution)/shard_map/ppermute | solution.py:28
  11.1 56.5 %collective-permute-start.1 = (f32[3,11,3,32]{3,1,2,0:T(8,128)S(1)}, f32[3,11,3,32]{3,1,2,0:T(8,128)S(1)}, u32[]{:S(2)}, u32[]{:S(2)}) collective-permute-start(f32[3,11,3,32]{3,1,2,0:T(8,128)S(1)} %get-tuple-element.35), channel_id=1, source_target_pairs={{1,0},{2,1},{3,2},{4,3},{5,4},{6,5},{7,6},{8,7},{9,8},{10,9},{11,1... | collective-permute-start | bytes 38024 | tf_op jit(solution)/shard_map/ppermute | solution.py:30
  18.5 33.8 %collective-permute-start.14 = (s32[256]{0:T(256)}, s32[256]{0:T(256)}, u32[]{:S(2)}, u32[]{:S(2)}) collective-permute-start(s32[256]{0:T(256)} %get-tuple-element.47), channel_id=1, source_target_pairs={{0,28},{1,29},{2,30},{3,31},{4,0},{5,1},{6,2},{7,3},{8,4},{9,5},{1... | collective-permute-start | bytes 3080 | tf_op jit(solution)/shard_map/ppermute | solution.py:39
  20.7 34.0 %collective-permute-start.15 = (s32[256]{0:T(256)}, s32[256]{0:T(256)}, u32[]{:S(2)}, u32[]{:S(2)}) collective-permute-start(s32[256]{0:T(256)} %get-tuple-element.46), channel_id=1, source_target_pairs={{0,29},{1,30},{2,31},{3,0},{4,1},{5,2},{6,3},{7,4},{8,5},{9,6},{10... | collective-permute-start | bytes 3080 | tf_op jit(solution)/shard_map/ppermute | solution.py:39
  20.7 34.7 %collective-permute-start.16 = (s32[256]{0:T(256)}, s32[256]{0:T(256)}, u32[]{:S(2)}, u32[]{:S(2)}) collective-permute-start(s32[256]{0:T(256)} %get-tuple-element.45), channel_id=1, source_target_pairs={{0,30},{1,31},{2,0},{3,1},{4,2},{5,3},{6,4},{7,5},{8,6},{9,7},{10,... | collective-permute-start | bytes 3080 | tf_op jit(solution)/shard_map/ppermute | solution.py:39
  24.6 64.2 %copy-start.23 = (s32[12288]{0:T(1024)}, s32[12288]{0:T(1024)S(1)}, u32[]{:S(2)}) copy-start(s32[12288]{0:T(1024)S(1)} %broadcast_clamp_fusion) | copy-start | bytes 147460
  25.6 22.3 %copy-start.42 = (f32[1,4096]{1,0:T(1,128)}, f32[1,4096]{1,0:T(1,128)S(1)}, u32[]{:S(2)}) copy-start(f32[1,4096]{1,0:T(1,128)S(1)} %get-tuple-element.39) | copy-start | bytes 49156
  25.7 22.3 %copy-start.45 = (f32[1,4096]{1,0:T(1,128)}, f32[1,4096]{1,0:T(1,128)S(1)}, u32[]{:S(2)}) copy-start(f32[1,4096]{1,0:T(1,128)S(1)} %get-tuple-element.40) | copy-start | bytes 49156
  25.7 22.3 %copy-start.48 = (f32[1,4096]{1,0:T(1,128)}, f32[1,4096]{1,0:T(1,128)S(1)}, u32[]{:S(2)}) copy-start(f32[1,4096]{1,0:T(1,128)S(1)} %get-tuple-element.41) | copy-start | bytes 49156
  25.7 22.3 %copy-start.51 = (f32[1,4096]{1,0:T(1,128)}, f32[1,4096]{1,0:T(1,128)S(1)}, u32[]{:S(2)}) copy-start(f32[1,4096]{1,0:T(1,128)S(1)} %get-tuple-element.42) | copy-start | bytes 49156
  52.3 5.3 collective-permute-start.17
  54.7 6.6 collective-permute-start.18
  55.4 7.2 collective-permute-start.19
  57.5 5.7 collective-permute-start.20
  61.3 6.3 collective-permute-start.21
  218.3 8.5 %copy-start.34 = (f32[66,3,11,1]{0,2,1,3:T(8,128)S(1)}, f32[66,3,11,1]{0,2,1,3:T(8,128)}, u32[]{:S(2)}) copy-start(f32[66,3,11,1]{0,2,1,3:T(8,128)} %copy-done.33) | copy-start | bytes 26140
  238.5 8.2 %copy-start.43 = (f32[1,4096]{1,0:T(1,128)S(1)}, f32[1,4096]{1,0:T(1,128)}, u32[]{:S(2)}) copy-start(f32[1,4096]{1,0:T(1,128)} %copy-done.42) | copy-start | bytes 49156
  238.5 8.2 %copy-start.46 = (f32[1,4096]{1,0:T(1,128)S(1)}, f32[1,4096]{1,0:T(1,128)}, u32[]{:S(2)}) copy-start(f32[1,4096]{1,0:T(1,128)} %copy-done.45) | copy-start | bytes 49156
  238.5 8.2 %copy-start.49 = (f32[1,4096]{1,0:T(1,128)S(1)}, f32[1,4096]{1,0:T(1,128)}, u32[]{:S(2)}) copy-start(f32[1,4096]{1,0:T(1,128)} %copy-done.48) | copy-start | bytes 49156
  238.5 8.2 %copy-start.52 = (f32[1,4096]{1,0:T(1,128)S(1)}, f32[1,4096]{1,0:T(1,128)}, u32[]{:S(2)}) copy-start(f32[1,4096]{1,0:T(1,128)} %copy-done.51) | copy-start | bytes 49156
  241.3 7.7 collective-permute-start.2
  241.3 8.3 %collective-permute-start.3 = (f32[3,11,3,32]{3,1,2,0:T(8,128)S(1)}, f32[3,11,3,32]{3,1,2,0:T(8,128)}, u32[]{:S(2)}, u32[]{:S(2)}) collective-permute-start(f32[3,11,3,32]{3,1,2,0:T(8,128)S(1)} %get-tuple-element.33), channel_id=1, source_target_pairs={{1,0},{2,1},{3,2},{4,3},{5,4},{6,5},{7,6},{8,7},{9,8},{10,9},{11,1... | collective-permute-start | bytes 38024 | tf_op jit(solution)/shard_map/ppermute | solution.py:30
  417.6 10.2 %copy-start.3 = (f32[3,66,4096]{2,1,0:T(8,128)}, f32[3,66,4096]{2,1,0:T(8,128)S(1)}, u32[]{:S(2)}) copy-start(f32[3,66,4096]{2,1,0:T(8,128)S(1)} %fusion.12) | copy-start | bytes 9732100
  428.2 8.2 %copy-start.44 = (f32[1,4096]{1,0:T(1,128)S(1)}, f32[1,4096]{1,0:T(1,128)}, u32[]{:S(2)}) copy-start(f32[1,4096]{1,0:T(1,128)} %copy-done.42) | copy-start | bytes 49156
  428.2 8.2 %copy-start.47 = (f32[1,4096]{1,0:T(1,128)S(1)}, f32[1,4096]{1,0:T(1,128)}, u32[]{:S(2)}) copy-start(f32[1,4096]{1,0:T(1,128)} %copy-done.45) | copy-start | bytes 49156
  428.2 8.2 %copy-start.50 = (f32[1,4096]{1,0:T(1,128)S(1)}, f32[1,4096]{1,0:T(1,128)}, u32[]{:S(2)}) copy-start(f32[1,4096]{1,0:T(1,128)} %copy-done.48) | copy-start | bytes 49156
  428.3 8.2 %copy-start.53 = (f32[1,4096]{1,0:T(1,128)S(1)}, f32[1,4096]{1,0:T(1,128)}, u32[]{:S(2)}) copy-start(f32[1,4096]{1,0:T(1,128)} %copy-done.51) | copy-start | bytes 49156
  431.0 7.7 collective-permute-start.4
  431.1 8.3 %collective-permute-start.5 = (f32[3,11,3,32]{3,1,2,0:T(8,128)S(1)}, f32[3,11,3,32]{3,1,2,0:T(8,128)}, u32[]{:S(2)}, u32[]{:S(2)}) collective-permute-start(f32[3,11,3,32]{3,1,2,0:T(8,128)S(1)} %get-tuple-element.31), channel_id=1, source_target_pairs={{1,0},{2,1},{3,2},{4,3},{5,4},{6,5},{7,6},{8,7},{9,8},{10,9},{11,1... | collective-permute-start | bytes 38024 | tf_op jit(solution)/shard_map/ppermute | solution.py:30
  611.6 8.3 %copy-start.54 = (s32[8192]{0:T(1024)S(1)}, s32[8192]{0:T(1024)}, u32[]{:S(2)}) copy-start(s32[8192]{0:T(1024)} %fusion.54) | copy-start | bytes 98308
  682.9 15.5 %copy-start.7 = (f32[64,66,66,1]{2,0,1,3:T(8,128)S(1)}, f32[64,66,66,1]{2,0,1,3:T(8,128)}, u32[]{:S(2)}) copy-start(f32[64,66,66,1]{2,0,1,3:T(8,128)} %select_bitcast_fusion.3) | copy-start | bytes 3345412
  682.9 15.5 %copy-start.61 = (pred[64,128]{1,0:T(8,128)(4,1)S(1)}, pred[64,128]{1,0:T(8,128)(4,1)}, u32[]{:S(2)}) copy-start(pred[64,128]{1,0:T(8,128)(4,1)} %and_bitcast_fusion) | copy-start | bytes 24580
  682.9 15.5 %copy-start.62 = (f32[8192]{0:T(1024)S(1)}, f32[8192]{0:T(1024)}, u32[]{:S(2)}) copy-start(f32[8192]{0:T(1024)} %param.29) | copy-start | bytes 98308
  725.3 7.7 collective-permute-start.6
  725.4 10.3 %collective-permute-start.7 = (f32[3,66,256]{2,1,0:T(8,128)S(1)}, f32[3,66,256]{2,1,0:T(8,128)S(1)}, u32[]{:S(2)}, u32[]{:S(2)}) collective-permute-start(f32[3,66,256]{2,1,0:T(8,128)S(1)} %get-tuple-element.18), channel_id=1, source_target_pairs={{0,29},{1,30},{2,31},{3,0},{4,1},{5,2},{6,3},{7,4},{8,5},{9,6},{10... | collective-permute-start | bytes 608264 | tf_op jit(solution)/shard_map/ppermute | solution.py:39
  725.4 39.2 %collective-permute-start.9 = (f32[3,66,1024]{2,1,0:T(8,128)S(1)}, f32[3,66,1024]{2,1,0:T(8,128)S(1)}, u32[]{:S(2)}, u32[]{:S(2)}) collective-permute-start(f32[3,66,1024]{2,1,0:T(8,128)S(1)} %get-tuple-element.21), channel_id=1, source_target_pairs={{0,31},{1,0},{2,1},{3,2},{4,3},{5,4},{6,5},{7,6},{8,7},{9,8},{10,9... | collective-permute-start | bytes 2433032 | tf_op jit(solution)/shard_map/ppermute | solution.py:39
  730.1 34.6 %collective-permute-start.10 = (f32[3,66,1024]{2,1,0:T(8,128)S(1)}, f32[3,66,1024]{2,1,0:T(8,128)S(1)}, u32[]{:S(2)}, u32[]{:S(2)}) collective-permute-start(f32[3,66,1024]{2,1,0:T(8,128)S(1)} %get-tuple-element.20), channel_id=1, source_target_pairs={{0,1},{1,2},{2,3},{3,4},{4,5},{5,6},{6,7},{7,8},{8,9},{9,10},{10,1... | collective-permute-start | bytes 2433032 | tf_op jit(solution)/shard_map/ppermute | solution.py:39
  732.5 23.2 %collective-permute-start.8 = (f32[3,66,256]{2,1,0:T(8,128)S(1)}, f32[3,66,256]{2,1,0:T(8,128)S(1)}, u32[]{:S(2)}, u32[]{:S(2)}) collective-permute-start(f32[3,66,256]{2,1,0:T(8,128)S(1)} %get-tuple-element.17), channel_id=1, source_target_pairs={{0,30},{1,31},{2,0},{3,1},{4,2},{5,3},{6,4},{7,5},{8,6},{9,7},{10,... | collective-permute-start | bytes 608264 | tf_op jit(solution)/shard_map/ppermute | solution.py:39
  733.0 31.8 %collective-permute-start.11 = (f32[3,66,256]{2,1,0:T(8,128)S(1)}, f32[3,66,256]{2,1,0:T(8,128)S(1)}, u32[]{:S(2)}, u32[]{:S(2)}) collective-permute-start(f32[3,66,256]{2,1,0:T(8,128)S(1)} %get-tuple-element.16), channel_id=1, source_target_pairs={{0,2},{1,3},{2,4},{3,5},{4,6},{5,7},{6,8},{7,9},{8,10},{9,11},{10,... | collective-permute-start | bytes 608264 | tf_op jit(solution)/shard_map/ppermute | solution.py:39
  735.6 29.2 %collective-permute-start.12 = (f32[3,66,256]{2,1,0:T(8,128)S(1)}, f32[3,66,256]{2,1,0:T(8,128)S(1)}, u32[]{:S(2)}, u32[]{:S(2)}) collective-permute-start(f32[3,66,256]{2,1,0:T(8,128)S(1)} %get-tuple-element.15), channel_id=1, source_target_pairs={{0,3},{1,4},{2,5},{3,6},{4,7},{5,8},{6,9},{7,10},{8,11},{9,12},{10... | collective-permute-start | bytes 608264 | tf_op jit(solution)/shard_map/ppermute | solution.py:39
  755.7 12.6 %collective-permute-start.13 = (f32[3,66,256]{2,1,0:T(8,128)S(1)}, f32[3,66,256]{2,1,0:T(8,128)S(1)}, u32[]{:S(2)}, u32[]{:S(2)}) collective-permute-start(f32[3,66,256]{2,1,0:T(8,128)S(1)} %get-tuple-element.14), channel_id=1, source_target_pairs={{0,4},{1,5},{2,6},{3,7},{4,8},{5,9},{6,10},{7,11},{8,12},{9,13},{1... | collective-permute-start | bytes 608264 | tf_op jit(solution)/shard_map/ppermute | solution.py:39
  768.4 35.1 %copy-start.1 = (f32[16,66,66]{2,0,1:T(8,128)S(1)}, f32[16,66,66]{2,0,1:T(8,128)}, u32[]{:S(2)}) copy-start(f32[16,66,66]{2,0,1:T(8,128)} %param.26) | copy-start | bytes 836356
  (43 other events, 155.7 us)
where the time goes:
time: 814 us; the launch traced here: 804 us
  local copies, waits for them, and re-layouts  587 us (72%)
  matrix products  114 us (14%)
  starting transfers between devices  43.4 us (5%)
  waiting for transfers between devices  31 us (4%)
  other arithmetic  26 us (3%)
    gather x6, local copies, waits for them, and re-layouts, advance(): outside = jnp.take(flattened, flat_index, axis=2)  350 us
    gather x2, local copies, waits for them, and re-layouts, body(): picked = jnp.take(adj_new, intersection_elem, axis=2)  78.5 us
    reshape x3, local copies, waits for them, and re-layouts, advance(): flattened = traces_wide.reshape(3, traces_wide.shape[1], -1)  56 us
    rev x3, local copies, waits for them, and re-layouts, advance(): jump_terms = traces - outside[:, ::-1]  45.8 us
    dot_general x1, matrix products, body(): jnp.dot(received, selector, precision=highest, preferred_element_type=jnp...  35.1 us
    ppermute x16, waiting for transfers between devices, shifted(): lax.ppermute(shard, axis, [(i, (i + by) % length) for i in range(length)])  31 us
    dot_general x3, matrix products, advance(): jnp.einsum('gnp,fnge->fpe', face_ones, jump_terms, precision=highest)  27.9 us
    ppermute x16, starting transfers between devices, shifted(): lax.ppermute(shard, axis, [(i, (i + by) % length) for i in range(length)])  26.1 us
  transfers between devices with their start and end apart: 22, of which 7 were waited for; matrix products, arithmetic and copies ran while one was open for 5% of the time, Pallas kernels for 0%

commit v1 on v0

v1 whole, which is shorter than its diff:
```python
import jax
import jax.numpy as jnp
import numpy as np
from jax import lax
from jax.sharding import PartitionSpec as P

ORDER = 10
REACH = 4
BLOCK = 128
RIM = 32
HALO = 128
E_OLD_DEV = 2048

gravity = 2.0
depth = 0.5
wave_speed = 1.0
time_step = 0.04
highest = lax.Precision.HIGHEST
AXES = ("gx", "gy")


def extended(cells, width):
    count = lax.axis_size(AXES)
    head = cells[:width]
    tail = cells[cells.shape[0] - width :]
    return jnp.concatenate(
        [
            lax.ppermute(tail, AXES, [(i, (i + 1) % count) for i in range(count)]),
            cells,
            lax.ppermute(head, AXES, [((i + 1) % count, i) for i in range(count)]),
        ],
        axis=0,
    )


def shifted(shard, by):
    length = lax.axis_size(AXES)
    return lax.ppermute(shard, AXES, [(i, (i + by) % length) for i in range(length)])


def face_table(degree):
    basis_count = (degree + 1) * (degree + 2) // 2

    def node_place(column, level):
        return level * (degree + 1) - level * (level - 1) // 2 + column

    ones_table = np.zeros((3, degree + 1, basis_count), np.float32)
    for level in range(degree + 1):
        ones_table[0, level, node_place(level, 0)] = 1.0
        ones_table[1, level, node_place(degree - level, level)] = 1.0
        ones_table[2, level, node_place(0, degree - level)] = 1.0
    return ones_table


def surface_matrix(degree):
    ones_table = face_table(degree)
    faces, nodes, basis_count = ones_table.shape
    own = ones_table.reshape(faces * nodes, basis_count)
    other = -ones_table[:, ::-1, :].reshape(faces * nodes, basis_count)
    return jnp.asarray(np.concatenate([own, other], axis=0))


def group_bounds(q_rows, reach):
    cap_far = q_rows // 32
    cap_near = q_rows // 8
    cap_home = q_rows - 2 * cap_near - 2 * (reach - 1) * cap_far
    bounds = []
    start = 0
    for offset in range(-reach, reach + 1):
        if offset == 0:
            group_size = cap_home
        elif abs(offset) == 1:
            group_size = cap_near
        else:
            group_size = cap_far
        bounds.append((offset, start, group_size))
        start = start + group_size
    return bounds


def split_dot(onehot, values):
    return jnp.dot(onehot.astype(jnp.float32), values, precision=lax.Precision.HIGH)


def body(
    adjoint,
    deriv_r,
    deriv_s,
    lift,
    metric,
    face_scale,
    face_angle,
    neighbours,
    neighbour_face,
    remap_table,
    intersection_elem,
    intersection_old,
    intersection_weight,
    block_type,
):
    fields, basis_count, elem_count = adjoint.shape
    nodes = ORDER + 1
    devices = lax.axis_size(AXES)
    elem_total = elem_count * devices
    first_elem = lax.axis_index(AXES) * elem_count
    width = elem_count + 2 * HALO

    state = adjoint.reshape(fields * basis_count, elem_count).T
    params = jnp.concatenate([metric, face_scale, face_angle], axis=0).T
    links = jnp.concatenate([neighbours, neighbour_face], axis=0).T
    both = extended(jnp.concatenate([state, params], axis=1), HALO)
    links = extended(links, HALO)
    start = both[:, : fields * basis_count]
    params = both[:, fields * basis_count :]
    m0, m1, m2, m3 = (params[:, k : k + 1] for k in range(4))
    half_scale = 0.5 * params[:, 4:7][:, :, None]
    angle = params[:, 7:10][:, :, None]
    normal_x = jnp.cos(angle)
    normal_y = jnp.sin(angle)
    local_index = (links[:, 0:3] - first_elem + HALO + elem_total) % elem_total
    local_index = jnp.clip(local_index, 0, width - 1)
    across_face = links[:, 3:6][:, :, None, None]

    mats = jnp.concatenate([deriv_r, deriv_s, lift], axis=1)
    surf = surface_matrix(ORDER)

    def advance(current):
        cur = current.reshape(width, fields, basis_count)
        prod = jnp.einsum("wcp,pk->wck", cur, mats, precision=highest)
        along_r = prod[:, :, :basis_count]
        along_s = prod[:, :, basis_count : 2 * basis_count]
        lifted = prod[:, :, 2 * basis_count :].reshape(width, fields, 3, nodes)
        to_height = -gravity * (
            m0 * along_r[:, 1] + m1 * along_s[:, 1] + m2 * along_r[:, 2] + m3 * along_s[:, 2]
        )
        to_along_x = -depth * (m0 * along_r[:, 0] + m1 * along_s[:, 0])
        to_along_y = -depth * (m2 * along_r[:, 0] + m3 * along_s[:, 0])
        height, along_x, along_y = (lifted[:, 0], lifted[:, 1], lifted[:, 2])
        face_height = half_scale * (
            gravity * (normal_x * along_x + normal_y * along_y) - wave_speed * height
        )
        face_along_x = half_scale * (depth * normal_x * height - wave_speed * along_x)
        face_along_y = half_scale * (depth * normal_y * height - wave_speed * along_y)
        traces = jnp.stack([face_height, face_along_x, face_along_y], axis=1)
        rows = traces.reshape(width, fields * 3 * nodes)
        picked = jnp.take(rows, local_index, axis=0).reshape(width, 3, fields, 3, nodes)
        outside = jnp.where(
            across_face == 0,
            picked[:, :, :, 0],
            jnp.where(across_face == 1, picked[:, :, :, 1], picked[:, :, :, 2]),
        )
        outside = jnp.swapaxes(outside, 1, 2).reshape(width, fields, 3 * nodes)
        jumps = jnp.concatenate([traces.reshape(width, fields, 3 * nodes), outside], axis=2)
        surface = jnp.einsum("wcn,np->wcp", jumps, surf, precision=highest)
        volume = jnp.stack([to_height, to_along_x, to_along_y], axis=1)
        return current + time_step * (volume + surface).reshape(width, fields * basis_count)

    section_two = 2.0 / 3.0 * advance(start)
    section_one = 0.25 * advance(section_two)
    adj_rows = start / 3.0 + 0.75 * section_two + advance(section_one)
    adj_rows = adj_rows[HALO : HALO + elem_count]
    adj_new = adj_rows.T.reshape(fields, basis_count, elem_count)

    rows_here = intersection_elem.shape[0]
    block_here = rows_here // BLOCK
    field_rows = fields * basis_count
    picked = jnp.take(adj_rows, intersection_elem, axis=0)
    picked = picked.reshape(block_here, BLOCK, fields, basis_count)
    chosen = jnp.take(remap_table, block_type, axis=0)
    mapped = jnp.einsum("brci,bij->brcj", picked, chosen, precision=highest)
    mapped = mapped * intersection_weight.reshape(block_here, BLOCK, 1, 1)
    mapped = mapped.reshape(rows_here, field_rows)
    labelled = jnp.concatenate(
        [mapped, intersection_old.astype(jnp.float32)[:, None]], axis=1
    )
    bounds = group_bounds(rows_here, REACH)
    kept = []
    for offset, start_row, group_size in bounds:
        piece = labelled[start_row : start_row + group_size]
        kept.append(piece if offset == 0 else shifted(piece, offset))
    received = jnp.concatenate(kept, axis=0)
    labels = received[:, field_rows].astype(jnp.int32)
    old_count = E_OLD_DEV
    selector = (jnp.arange(old_count, dtype=jnp.int32)[:, None] == labels[None, :])
    old_sums = split_dot(selector, received[:, :field_rows])
    return (adj_new, old_sums.T.reshape(fields, basis_count, old_count))


def solution(mesh):
    in_specs = (
        P(None, None, AXES),
        P(),
        P(),
        P(),
        P(None, AXES),
        P(None, AXES),
        P(None, AXES),
        P(None, AXES),
        P(None, AXES),
        P(),
        P(AXES),
        P(AXES),
        P(AXES),
        P(AXES),
    )
    out_specs = (P(None, None, AXES), P(None, None, AXES))
    return jax.shard_map(body, mesh=mesh, in_specs=in_specs, out_specs=out_specs, check_vma=False)
```

time: 814 us -> 586 us (0.72)
  local copies, waits for them, and re-layouts: 587 us -> 313 us
  other arithmetic: 26 us -> 111 us
  starting transfers between devices: 43.4 us -> 20.4 us
  matrix products: 114 us -> 104 us
    gather x8, local copies, waits for them, and re-layouts: 428 us -> 150 us  [the longest x6 107 us: advance(): jnp.take(rows, local_index, axis=0).reshape(width, 3, fields, 3, nodes)]
    rev x3 -> x0, local copies, waits for them, and re-layouts: 45.8 us -> none  [advance(): jump_terms = traces - outside[:, ::-1]]
    select_n x3 -> x4, other arithmetic: 8.64 us -> 47.8 us  [the longest x3 46.3 us: advance(): jnp.take(rows, local_index, axis=0).reshape(width, 3, fields, 3, nodes)]
    select_n x0 -> x4, local copies, waits for them, and re-layouts: none -> 29.8 us  [advance(): jnp.take(rows, local_index, axis=0).reshape(width, 3, fields, 3, nodes)]
    ppermute x22 -> x12, starting transfers between devices: 43.4 us -> 20.4 us  [the longest x2 11.8 us: extended(): lax.ppermute(head, AXES, [((i + 1) % count, i) for i in range(count)])]
    another operation x0 -> x9, local copies, waits for them, and re-layouts: none -> 19 us  [advance(): traces = jnp.stack([face_height, face_along_x, face_along_y], axis=1)]
    mul x8 -> x9, other arithmetic: 10.8 us -> 26 us  [the longest x3 9.39 us: advance(): -gravity]
    concatenate x5 -> x1, local copies, waits for them, and re-layouts: 11.1 us -> 0.01 us  [body(): received = jnp.concatenate(kept, axis=0)]
  transfers between devices with their start and end apart: 22 -> 12, of which waited for: 7 -> 5; matrix products, arithmetic and copies ran while one was open for 5% -> 3% of each run, Pallas kernels for 0% -> 0%
where the time goes in v1:
time: 586 us; the launch traced here: 579 us
  local copies, waits for them, and re-layouts  313 us (53%)
  other arithmetic  111 us (19%)
  matrix products  104 us (18%)
  waiting for transfers between devices  28.3 us (5%)
  starting transfers between devices  20.4 us (3%)
    gather x6, local copies, waits for them, and re-layouts, advance(): jnp.take(rows, local_index, axis=0).reshape(width, 3, fields, 3, nodes)  107 us
    select_n x3, other arithmetic, advance(): jnp.take(rows, local_index, axis=0).reshape(width, 3, fields, 3, nodes)  46.3 us
    gather x2, local copies, waits for them, and re-layouts, body(): picked = jnp.take(adj_rows, intersection_elem, axis=0)  42.8 us
    dot_general x3, matrix products, advance(): surface = jnp.einsum('wcn,np->wcp', jumps, surf, precision=highest)  34.1 us
    select_n x4, local copies, waits for them, and re-layouts, advance(): jnp.take(rows, local_index, axis=0).reshape(width, 3, fields, 3, nodes)  29.8 us
    dot_general x3, matrix products, advance(): prod = jnp.einsum('wcp,pk->wck', cur, mats, precision=highest)  28.7 us
    ppermute x8, waiting for transfers between devices, shifted(): lax.ppermute(shard, AXES, [(i, (i + by) % length) for i in range(length)])  28.3 us
    dot_general x1, matrix products, split_dot(): jnp.dot(onehot.astype(jnp.float32), values, precision=lax.Precision.HIGH)  26 us
  transfers between devices with their start and end apart: 12, of which 5 were waited for; matrix products, arithmetic and copies ran while one was open for 3% of the time, Pallas kernels for 0%

profile of v1, /device:TPU:0, one launch (start us, length us, event | category | flops | bytes accessed | tf_op | source)
XLA Modules:
  0.0 578.6 jit_solution(17113498950981970939)
XLA Ops:
  0.7 4.2 reshape.270
  6.6 6.4 %collective-permute-start.1 = (f32[128,208]{0,1:T(8,128)}, f32[128,208]{0,1:T(8,128)S(1)}, u32[]{:S(2)}, u32[]{:S(2)}) collective-permute-start(f32[128,208]{0,1:T(8,128)} %get-tuple-element.34), channel_id=1, source_target_pairs={{1,0},{2,1},{3,2},{4,3},{5,4},{6,5},{7,6},{8,7},{9,8},{10,9},{11,1... | collective-permute-start | bytes 319496 | tf_op jit(solution)/shard_map/ppermute | solution.py:30
  13.1 5.4 collective-permute-start.3
  19.1 4.6 gather_fusion.1
  36.6 4.2 reshape.271
  40.8 9.8 %fusion.66 = f32[4352,3,165]{0,2,1:T(8,128)S(1)} fusion(f32[4352,3,66]{0,2,1:T(8,128)} %reshape.271, f32[66,33]{1,0:T(8,128)S(1)} %copy.146, f32[66,66]{1,0:T(8,128)S(1)} %copy-done.14, f32[66,66]{1,0:T(8,128)S(1)} %copy-done.15), kind=kOutput, calls=%fused_computation.174 | convolution fusion | flops 1706179840 | bytes 12107304 | tf_op jit(solution)/shard_map/wcp,pk->wck/dot_general | solution.py:129
  71.4 24.8 %gather_fusion.2 = f32[13056,99]{1,0:T(8,128)} fusion(f32[4352,99]{1,0:T(8,128)S(1)} %copy.152, s32[13312]{0:T(1024)S(1)} %pad_clamp_fusion), kind=kCustom, calls=%fused_computation.clone | custom fusion | bytes 10392576 | tf_op jit(solution)/shard_map/jit(_take)/gather | solution.py:146
  96.2 11.0 %reshape.340 = f32[4352,3,99]{2,1,0:T(4,128)} reshape(f32[13056,99]{1,0:T(8,128)} %gather_fusion.2) | data formatting | bytes 10340352 | tf_op jit(solution)/shard_map/jit(_take)/gather | solution.py:146
  107.2 15.4 %broadcast_select_fusion.2 = f32[4352,3,99]{2,1,0:T(4,128)} fusion(f32[4352,3,99]{2,1,0:T(4,128)} %reshape.340, pred[4352,3]{1,0:T(8,128)(4,1)S(1)} %copy-done.6), kind=kLoop, calls=%fused_computation.27 | loop fusion | flops 1292544 | bytes 10353408 | tf_op jit(solution)/shard_map/jit(_take)/select_n | solution.py:146
  122.6 9.6 %copy.153 = f32[4352,3,99]{0,2,1:T(8,128)} copy(f32[4352,3,99]{2,1,0:T(4,128)} %broadcast_select_fusion.2) | data formatting | bytes 10340352 | tf_op jit(solution)/shard_map/jit(_take)/select_n | solution.py:146
  132.2 6.3 %reshape.274 = f32[4352,3,3,3,11]{0,4,3,2,1:T(8,128)} reshape(f32[4352,3,99]{0,2,1:T(8,128)} %copy.153) | data formatting | bytes 10340352 | tf_op jit(solution)/shard_map/reshape | solution.py:146
  138.6 3.6 fusion.43
  145.3 4.3 fusion.54
  149.7 14.9 %fusion.6 = f32[4352,3,66]{0,2,1:T(8,128)} fusion(f32[66,66,1]{0,1,2:T(8,128)S(1)} %copy-done.36, f32[4352,1,66]{0,2,1:T(8,128)S(1)} %get-tuple-element.23, f32[4352,1,66]{0,2,1:T(8,128)S(1)} %get-tuple-element.22, f32[4352,1,66]{0,2,1:T(8,128)S(1)} %get-tuple-element.21, f32[4352,3,33]{0,2,1:T(8,128)S(1)} %copy-done.9, f32[4352,1,33]{0,2,1:T(8,128)S(1)} %copy-done.10, ...), kind=kOutput, calls=%fused_computation.19 | convolution fusion | flops 688495104 | bytes 10357776 | tf_op jit(solution)/shard_map/wcn,np->wcp/dot_general | solution.py:154
  164.6 4.2 mul.483
  168.9 6.4 %broadcast_multiply_fusion.1 = (f32[4352,198]{0,1:T(8,128)}, f32[4352,198]{0,1:T(8,128)}) fusion(f32[4352,198]{0,1:T(8,128)} %mul.483, f32[4352,208]{0,1:T(8,128)} %copy-done.4), kind=kLoop, calls=%fused_computation.83 | loop fusion | flops 1723392 | bytes 13787136 | tf_op jit(solution)/shard_map/mul | solution.py:158
  175.3 4.2 reshape.276
  179.5 9.3 %fusion.65 = f32[4352,3,165]{0,2,1:T(8,128)S(1)} fusion(f32[4352,3,66]{0,2,1:T(8,128)} %reshape.276, f32[66,33]{1,0:T(8,128)S(1)} %copy.146, f32[66,66]{1,0:T(8,128)S(1)} %copy-done.14, f32[66,66]{1,0:T(8,128)S(1)} %copy-done.15), kind=kOutput, calls=%fused_computation.173 | convolution fusion | flops 1706179840 | bytes 12107304 | tf_op jit(solution)/shard_map/wcp,pk->wck/dot_general | solution.py:129
  207.8 24.8 %gather_fusion.3 = f32[13056,99]{1,0:T(8,128)} fusion(f32[4352,99]{1,0:T(8,128)S(1)} %copy.162, s32[13312]{0:T(1024)S(1)} %pad_clamp_fusion), kind=kCustom, calls=%fused_computation.1.clone | custom fusion | bytes 10392576 | tf_op jit(solution)/shard_map/jit(_take)/gather | solution.py:146
  232.6 11.0 %reshape.344 = f32[4352,3,99]{2,1,0:T(4,128)} reshape(f32[13056,99]{1,0:T(8,128)} %gather_fusion.3) | data formatting | bytes 10340352 | tf_op jit(solution)/shard_map/jit(_take)/gather | solution.py:146
  243.6 15.4 %broadcast_select_fusion.1 = f32[4352,3,99]{2,1,0:T(4,128)} fusion(f32[4352,3,99]{2,1,0:T(4,128)} %reshape.344, pred[4352,3]{1,0:T(8,128)(4,1)S(1)} %copy-done.7), kind=kLoop, calls=%fused_computation.26 | loop fusion | flops 1292544 | bytes 10353408 | tf_op jit(solution)/shard_map/jit(_take)/select_n | solution.py:146
  259.0 9.8 %copy.163 = f32[4352,3,99]{0,2,1:T(8,128)} copy(f32[4352,3,99]{2,1,0:T(4,128)} %broadcast_select_fusion.1) | data formatting | bytes 10340352 | tf_op jit(solution)/shard_map/jit(_take)/select_n | solution.py:146
  268.8 6.7 %reshape.279 = f32[4352,3,3,3,11]{0,4,3,2,1:T(8,128)} reshape(f32[4352,3,99]{0,2,1:T(8,128)} %copy.163) | data formatting | bytes 10340352 | tf_op jit(solution)/shard_map/reshape | solution.py:146
  281.0 9.6 %fusion.5 = f32[4352,3,66]{0,2,1:T(8,128)} fusion(f32[66,66,1]{0,1,2:T(8,128)S(1)} %copy-done.36, f32[4352,1,66]{0,2,1:T(8,128)} %get-tuple-element.20, f32[4352,1,66]{0,2,1:T(8,128)} %get-tuple-element.19, f32[4352,1,66]{0,2,1:T(8,128)} %get-tuple-element.18, f32[4352,3,33]{0,2,1:T(8,128)} %reshape.280, f32[4352,1,33]{0,2,1:T(8,128)} %stack.83, ...), kind=kOutput, calls=%fused_computation.17 | convolution fusion | flops 688495104 | bytes 10357776 | tf_op jit(solution)/shard_map/wcn,np->wcp/dot_general | solution.py:154
  290.6 4.2 mul.508
  294.9 5.3 add_multiply_fusion
  300.1 4.2 reshape.281
  304.3 9.5 %fusion.64 = f32[4352,3,165]{0,2,1:T(8,128)S(1)} fusion(f32[4352,3,66]{0,2,1:T(8,128)} %reshape.281, f32[66,33]{1,0:T(8,128)S(1)} %copy.146, f32[66,66]{1,0:T(8,128)S(1)} %copy-done.14, f32[66,66]{1,0:T(8,128)S(1)} %copy-done.15), kind=kOutput, calls=%fused_computation.172 | convolution fusion | flops 1706179840 | bytes 12107304 | tf_op jit(solution)/shard_map/wcp,pk->wck/dot_general | solution.py:129
  332.9 24.8 %gather_fusion.4 = f32[13056,99]{1,0:T(8,128)} fusion(f32[4352,99]{1,0:T(8,128)S(1)} %copy.173, s32[13312]{0:T(1024)S(1)} %pad_clamp_fusion), kind=kCustom, calls=%fused_computation.2.clone | custom fusion | bytes 10392576 | tf_op jit(solution)/shard_map/jit(_take)/gather | solution.py:146
  357.7 11.0 %reshape.348 = f32[4352,3,99]{2,1,0:T(4,128)} reshape(f32[13056,99]{1,0:T(8,128)} %gather_fusion.4) | data formatting | bytes 10340352 | tf_op jit(solution)/shard_map/jit(_take)/gather | solution.py:146
  368.7 15.4 %broadcast_select_fusion = f32[4352,3,99]{2,1,0:T(4,128)} fusion(f32[4352,3,99]{2,1,0:T(4,128)} %reshape.348, pred[4352,3]{1,0:T(8,128)(4,1)S(1)} %copy-done.8), kind=kLoop, calls=%fused_computation.25 | loop fusion | flops 1292544 | bytes 10353408 | tf_op jit(solution)/shard_map/jit(_take)/select_n | solution.py:146
  384.1 9.8 %copy.174 = f32[4352,3,99]{0,2,1:T(8,128)} copy(f32[4352,3,99]{2,1,0:T(4,128)} %broadcast_select_fusion) | data formatting | bytes 10340352 | tf_op jit(solution)/shard_map/jit(_take)/select_n | solution.py:146
  393.9 6.3 %reshape.284 = f32[4352,3,3,3,11]{0,4,3,2,1:T(8,128)} reshape(f32[4352,3,99]{0,2,1:T(8,128)} %copy.174) | data formatting | bytes 10340352 | tf_op jit(solution)/shard_map/reshape | solution.py:146
  405.6 9.6 %fusion.4 = f32[4352,3,66]{0,2,1:T(8,128)} fusion(f32[66,66,1]{0,1,2:T(8,128)S(1)} %copy-done.36, f32[4352,1,66]{0,2,1:T(8,128)} %get-tuple-element.17, f32[4352,1,66]{0,2,1:T(8,128)} %get-tuple-element.16, f32[4352,1,66]{0,2,1:T(8,128)} %get-tuple-element.15, f32[4352,3,33]{0,2,1:T(8,128)} %reshape.285, f32[4352,1,33]{0,2,1:T(8,128)} %stack.86, ...), kind=kOutput, calls=%fused_computation.15 | convolution fusion | flops 688495104 | bytes 10357776 | tf_op jit(solution)/shard_map/wcn,np->wcp/dot_general | solution.py:154
  415.2 4.2 mul.531
  419.4 8.0 %fusion.31 = f32[4096,198]{0,1:T(8,128)} fusion(f32[4352,198]{0,1:T(8,128)} %mul.531, f32[4352,198]{0,1:T(8,128)} %add_multiply_fusion, f32[4352,198]{0,1:T(8,128)} %get-tuple-element.10, f32[4352,198]{0,1:T(8,128)} %slice.315), kind=kLoop, calls=%fused_computation.55 | loop fusion | flops 4055040 | bytes 16220160 | tf_op jit(solution)/shard_map/add | solution.py:160
  427.4 5.3 copy.179
  432.7 33.7 %gather_fusion = f32[8192,198]{1,0:T(8,128)} fusion(f32[4096,198]{1,0:T(8,128)} %copy.179, s32[8192]{0:T(1024)S(1)} %copy-done.24), kind=kCustom, calls=%fused_computation.3 | custom fusion | bytes 13008896 | tf_op jit(solution)/shard_map/jit(_take)/gather | solution.py:167
  466.4 9.1 %copy.180 = f32[8192,198]{0,1:T(8,128)} copy(f32[8192,198]{1,0:T(8,128)} %gather_fusion) | data formatting | bytes 12976128 | tf_op jit(solution)/shard_map/jit(_take)/gather | solution.py:167
  475.5 4.1 copy.195
  482.4 15.5 %broadcast_multiply_fusion = f32[64,128,3,66]{1,3,2,0:T(8,128)S(1)} fusion(f32[64,128]{1,0:T(8,128)S(1)} %bitcast.177, f32[64,128,3,66]{1,0,3,2:T(8,128)S(1)} %broadcast_select_fusion.3, f32[64,66,66,1]{2,0,1,3:T(8,128)S(1)} %copy-done.5), kind=kOutput, calls=%fused_computation.52 | convolution fusion | flops 1286258688 | bytes 14124032 | tf_op jit(solution)/shard_map/brci,bij->brcj/dot_general | solution.py:170
  500.3 6.0 %copy.196 = f32[25,8,64,128]{3,1,2,0:T(8,128)S(1)} copy(f32[25,8,64,128]{3,2,1,0:T(8,128)S(1)} %bitcast.170) | data formatting | bytes 13107200
  506.4 5.4 collective-permute-start.7
  512.7 4.1 reshape.286
  519.4 12.8 %collective-permute-done.4 = f32[256,199]{0,1:T(8,128)S(1)} collective-permute-done((f32[256,199]{0,1:T(8,128)S(1)}, f32[256,199]{0,1:T(8,128)S(1)}, u32[]{:S(2)}, u32[]{:S(2)}) %collective-permute-start.4) | collective-permute-done | bytes 203808 | tf_op jit(solution)/shard_map/ppermute | solution.py:38
  539.9 5.0 collective-permute-done.9
  544.9 6.0 %collective-permute-done.11 = f32[256,199]{0,1:T(8,128)S(1)} collective-permute-done((f32[256,199]{0,1:T(8,128)S(1)}, f32[256,199]{0,1:T(8,128)S(1)}, u32[]{:S(2)}, u32[]{:S(2)}) %collective-permute-start.11) | collective-permute-done | bytes 203808 | tf_op jit(solution)/shard_map/ppermute | solution.py:38
  551.0 26.0 %fusion = f32[198,2048]{1,0:T(8,128)S(1)} fusion(s32[8192]{0:T(1024)S(1)} %bitcast.178, f32[8192,199]{0,1:T(8,128)S(1)} %constant_dynamic-update-slice_fusion), kind=kOutput, calls=%fused_computation.6 | convolution fusion | flops 19948109824 | bytes 8175616 | tf_op jit(solution)/shard_map/dot_general | solution.py:82
  (170 shorter events, 105.6 us)
Async XLA Ops:
  0.6 18.5 %copy-start = (f32[16,66,66]{2,0,1:T(8,128)S(1)}, f32[16,66,66]{2,0,1:T(8,128)}, u32[]{:S(2)}) copy-start(f32[16,66,66]{2,0,1:T(8,128)} %param.26) | copy-start | bytes 836356
  0.6 4.2 copy-start.26
  0.7 4.2 copy-start.27
  0.7 4.2 copy-start.28
  4.9 8.1 %copy-start.29 = (s32[3,4096]{1,0:T(4,128)S(1)}, s32[3,4096]{1,0:T(4,128)}, u32[]{:S(2)}) copy-start(s32[3,4096]{1,0:T(4,128)} %param.25) | copy-start | bytes 147460
  4.9 8.1 %copy-start.30 = (s32[3,4096]{1,0:T(4,128)S(1)}, s32[3,4096]{1,0:T(4,128)}, u32[]{:S(2)}) copy-start(s32[3,4096]{1,0:T(4,128)} %param.24) | copy-start | bytes 147460
  4.9 13.6 %copy-start.35 = (s32[64]{0:T(128)S(1)}, s32[64]{0:T(128)}, u32[]{:S(2)}) copy-start(s32[64]{0:T(128)} %param.30) | copy-start | bytes 772
  4.9 13.6 %copy-start.25 = (s32[8192]{0:T(1024)S(1)}, s32[8192]{0:T(1024)}, u32[]{:S(2)}) copy-start(s32[8192]{0:T(1024)} %param.27) | copy-start | bytes 98308
  6.6 24.0 %collective-permute-start.1 = (f32[128,208]{0,1:T(8,128)}, f32[128,208]{0,1:T(8,128)S(1)}, u32[]{:S(2)}, u32[]{:S(2)}) collective-permute-start(f32[128,208]{0,1:T(8,128)} %get-tuple-element.34), channel_id=1, source_target_pairs={{1,0},{2,1},{3,2},{4,3},{5,4},{6,5},{7,6},{8,7},{9,8},{10,9},{11,1... | collective-permute-start | bytes 319496 | tf_op jit(solution)/shard_map/ppermute | solution.py:30
  13.0 17.6 %collective-permute-start = (f32[128,208]{0,1:T(8,128)}, f32[128,208]{0,1:T(8,128)S(1)}, u32[]{:S(2)}, u32[]{:S(2)}) collective-permute-start(f32[128,208]{0,1:T(8,128)} %get-tuple-element.33), channel_id=1, source_target_pairs={{0,1},{1,2},{2,3},{3,4},{4,5},{5,6},{6,7},{7,8},{8,9},{9,10},{10,1... | collective-permute-start | bytes 319496 | tf_op jit(solution)/shard_map/ppermute | solution.py:28
  13.1 13.7 %collective-permute-start.3 = (s32[128,6]{0,1:T(8,128)S(1)}, s32[128,6]{0,1:T(8,128)S(1)}, u32[]{:S(2)}, u32[]{:S(2)}) collective-permute-start(s32[128,6]{0,1:T(8,128)S(1)} %get-tuple-element.49), channel_id=1, source_target_pairs={{1,0},{2,1},{3,2},{4,3},{5,4},{6,5},{7,6},{8,7},{9,8},{10,9},{11,1... | collective-permute-start | bytes 9224 | tf_op jit(solution)/shard_map/ppermute | solution.py:30
  18.4 8.3 %collective-permute-start.2 = (s32[128,6]{0,1:T(8,128)S(1)}, s32[128,6]{0,1:T(8,128)S(1)}, u32[]{:S(2)}, u32[]{:S(2)}) collective-permute-start(s32[128,6]{0,1:T(8,128)S(1)} %get-tuple-element.48), channel_id=1, source_target_pairs={{0,1},{1,2},{2,3},{3,4},{4,5},{5,6},{6,7},{7,8},{8,9},{9,10},{10,1... | collective-permute-start | bytes 9224 | tf_op jit(solution)/shard_map/ppermute | solution.py:28
  23.7 2.3 copy-start.34
  23.7 2.4 copy-start.32
  26.9 111.6 %copy-start.20 = (pred[4352,3]{0,1:T(4,128)(4,1)}, pred[4352,3]{0,1:T(4,128)(4,1)S(1)}, u32[]{:S(2)}) copy-start(pred[4352,3]{0,1:T(4,128)(4,1)S(1)} %get-tuple-element.44) | copy-start | bytes 39172
  26.9 111.6 %copy-start.22 = (pred[4352,3]{0,1:T(4,128)(4,1)}, pred[4352,3]{0,1:T(4,128)(4,1)S(1)}, u32[]{:S(2)}) copy-start(pred[4352,3]{0,1:T(4,128)(4,1)S(1)} %get-tuple-element.45) | copy-start | bytes 39172
  32.8 1.8 copy-start.4
  36.6 4.2 copy-start.14
  36.6 4.2 copy-start.15
  50.6 3.4 copy-start.3
  96.2 11.0 %copy-start.6 = (pred[4352,3]{1,0:T(8,128)(4,1)S(1)}, pred[4352,3]{1,0:T(8,128)(4,1)}, u32[]{:S(2)}) copy-start(pred[4352,3]{1,0:T(8,128)(4,1)} %copy.150) | copy-start | bytes 39172
  145.2 43.6 %copy-start.16 = (f32[4352]{0:T(1024)}, f32[4352]{0:T(1024)S(1)}, u32[]{:S(2)}) copy-start(f32[4352]{0:T(1024)S(1)} %get-tuple-element.7) | copy-start | bytes 52228
  145.2 43.6 %copy-start.18 = (f32[4352]{0:T(1024)}, f32[4352]{0:T(1024)S(1)}, u32[]{:S(2)}) copy-start(f32[4352]{0:T(1024)S(1)} %get-tuple-element.8) | copy-start | bytes 52228
  145.2 4.4 copy-start.9
  145.2 4.4 copy-start.10
  145.2 4.4 copy-start.11
  145.2 4.5 copy-start.12
  145.3 4.5 copy-start.36
  232.6 11.0 %copy-start.7 = (pred[4352,3]{1,0:T(8,128)(4,1)S(1)}, pred[4352,3]{1,0:T(8,128)(4,1)}, u32[]{:S(2)}) copy-start(pred[4352,3]{1,0:T(8,128)(4,1)} %copy.150) | copy-start | bytes 39172
  268.8 6.8 %copy-start.21 = (pred[4352,3]{0,1:T(4,128)(4,1)S(1)}, pred[4352,3]{0,1:T(4,128)(4,1)}, u32[]{:S(2)}) copy-start(pred[4352,3]{0,1:T(4,128)(4,1)} %copy-done.20) | copy-start | bytes 39172
  268.8 6.8 %copy-start.23 = (pred[4352,3]{0,1:T(4,128)(4,1)S(1)}, pred[4352,3]{0,1:T(4,128)(4,1)}, u32[]{:S(2)}) copy-start(pred[4352,3]{0,1:T(4,128)(4,1)} %copy-done.22) | copy-start | bytes 39172
  304.3 9.6 %copy-start.17 = (f32[4352]{0:T(1024)S(1)}, f32[4352]{0:T(1024)}, u32[]{:S(2)}) copy-start(f32[4352]{0:T(1024)} %copy-done.16) | copy-start | bytes 52228
  304.3 9.6 %copy-start.19 = (f32[4352]{0:T(1024)S(1)}, f32[4352]{0:T(1024)}, u32[]{:S(2)}) copy-start(f32[4352]{0:T(1024)} %copy-done.18) | copy-start | bytes 52228
  357.7 11.0 %copy-start.8 = (pred[4352,3]{1,0:T(8,128)(4,1)S(1)}, pred[4352,3]{1,0:T(8,128)(4,1)}, u32[]{:S(2)}) copy-start(pred[4352,3]{1,0:T(8,128)(4,1)} %copy.150) | copy-start | bytes 39172
  427.4 5.3 copy-start.24
  480.8 1.6 copy-start.5
  480.8 1.6 copy-start.31
  500.3 6.0 %copy-start.13 = (f32[8192]{0:T(1024)S(1)}, f32[8192]{0:T(1024)}, u32[]{:S(2)}) copy-start(f32[8192]{0:T(1024)} %convert_element_type.14) | copy-start | bytes 98308
  506.2 5.6 copy-start.2
  506.4 31.0 %collective-permute-start.7 = (f32[1024,199]{0,1:T(8,128)S(1)}, f32[1024,199]{0,1:T(8,128)S(1)}, u32[]{:S(2)}, u32[]{:S(2)}) collective-permute-start(f32[1024,199]{0,1:T(8,128)S(1)} %get-tuple-element.31), channel_id=1, source_target_pairs={{0,31},{1,0},{2,1},{3,2},{4,3},{5,4},{6,5},{7,6},{8,7},{9,8},{10,9... | collective-permute-start | bytes 2445320 | tf_op jit(solution)/shard_map/ppermute | solution.py:38
  512.7 19.5 %collective-permute-start.4 = (f32[256,199]{0,1:T(8,128)S(1)}, f32[256,199]{0,1:T(8,128)S(1)}, u32[]{:S(2)}, u32[]{:S(2)}) collective-permute-start(f32[256,199]{0,1:T(8,128)S(1)} %get-tuple-element.28), channel_id=1, source_target_pairs={{0,28},{1,29},{2,30},{3,31},{4,0},{5,1},{6,2},{7,3},{8,4},{9,5},{1... | collective-permute-start | bytes 611336 | tf_op jit(solution)/shard_map/ppermute | solution.py:38
  512.7 21.8 %collective-permute-start.5 = (f32[256,199]{0,1:T(8,128)}, f32[256,199]{0,1:T(8,128)S(1)}, u32[]{:S(2)}, u32[]{:S(2)}) collective-permute-start(f32[256,199]{0,1:T(8,128)} %get-tuple-element.27), channel_id=1, source_target_pairs={{0,29},{1,30},{2,31},{3,0},{4,1},{5,2},{6,3},{7,4},{8,5},{9,6},{10... | collective-permute-start | bytes 611336 | tf_op jit(solution)/shard_map/ppermute | solution.py:38
  516.8 19.9 %collective-permute-start.6 = (f32[256,199]{0,1:T(8,128)}, f32[256,199]{0,1:T(8,128)S(1)}, u32[]{:S(2)}, u32[]{:S(2)}) collective-permute-start(f32[256,199]{0,1:T(8,128)} %get-tuple-element.26), channel_id=1, source_target_pairs={{0,30},{1,31},{2,0},{3,1},{4,2},{5,3},{6,4},{7,5},{8,6},{9,7},{10,... | collective-permute-start | bytes 611336 | tf_op jit(solution)/shard_map/ppermute | solution.py:38
  517.3 22.5 %collective-permute-start.8 = (f32[1024,199]{0,1:T(8,128)S(1)}, f32[1024,199]{0,1:T(8,128)S(1)}, u32[]{:S(2)}, u32[]{:S(2)}) collective-permute-start(f32[1024,199]{0,1:T(8,128)S(1)} %get-tuple-element.30), channel_id=1, source_target_pairs={{0,1},{1,2},{2,3},{3,4},{4,5},{5,6},{6,7},{7,8},{8,9},{9,10},{10,1... | collective-permute-start | bytes 2445320 | tf_op jit(solution)/shard_map/ppermute | solution.py:38
  532.2 12.6 %collective-permute-start.9 = (f32[256,199]{0,1:T(8,128)}, f32[256,199]{0,1:T(8,128)S(1)}, u32[]{:S(2)}, u32[]{:S(2)}) collective-permute-start(f32[256,199]{0,1:T(8,128)} %get-tuple-element.25), channel_id=1, source_target_pairs={{0,2},{1,3},{2,4},{3,5},{4,6},{5,7},{6,8},{7,9},{8,10},{9,11},{10,... | collective-permute-start | bytes 611336 | tf_op jit(solution)/shard_map/ppermute | solution.py:38
  534.5 10.3 %collective-permute-start.10 = (f32[256,199]{0,1:T(8,128)}, f32[256,199]{0,1:T(8,128)S(1)}, u32[]{:S(2)}, u32[]{:S(2)}) collective-permute-start(f32[256,199]{0,1:T(8,128)} %get-tuple-element.29), channel_id=1, source_target_pairs={{0,3},{1,4},{2,5},{3,6},{4,7},{5,8},{6,9},{7,10},{8,11},{9,12},{10... | collective-permute-start | bytes 611336 | tf_op jit(solution)/shard_map/ppermute | solution.py:38
  536.7 14.2 %collective-permute-start.11 = (f32[256,199]{0,1:T(8,128)S(1)}, f32[256,199]{0,1:T(8,128)S(1)}, u32[]{:S(2)}, u32[]{:S(2)}) collective-permute-start(f32[256,199]{0,1:T(8,128)S(1)} %get-tuple-element.24), channel_id=1, source_target_pairs={{0,4},{1,5},{2,6},{3,7},{4,8},{5,9},{6,10},{7,11},{8,12},{9,13},{1... | collective-permute-start | bytes 611336 | tf_op jit(solution)/shard_map/ppermute | solution.py:38
  551.0 27.4 %copy-start.1 = (f32[16,66,66]{2,0,1:T(8,128)S(1)}, f32[16,66,66]{2,0,1:T(8,128)}, u32[]{:S(2)}) copy-start(f32[16,66,66]{2,0,1:T(8,128)} %param.26) | copy-start | bytes 836356
  (1 other events, 1.2 us)

commit v2 on v1

--- a/solution.py
+++ b/solution.py
@@ -2,6 +2,8 @@
 import jax.numpy as jnp
 import numpy as np
 from jax import lax
+from jax.experimental import pallas as pl
+from jax.experimental.pallas import tpu as pltpu
 from jax.sharding import PartitionSpec as P
 
 ORDER = 10
@@ -19,17 +21,18 @@
 AXES = ("gx", "gy")
 
 
-def extended(cells, width):
+def extended(cells, width, axis=0):
     count = lax.axis_size(AXES)
-    head = cells[:width]
-    tail = cells[cells.shape[0] - width :]
+    size = cells.shape[axis]
+    head = lax.slice_in_dim(cells, 0, width, axis=axis)
+    tail = lax.slice_in_dim(cells, size - width, size, axis=axis)
     return jnp.concatenate(
         [
             lax.ppermute(tail, AXES, [(i, (i + 1) % count) for i in range(count)]),
             cells,
             lax.ppermute(head, AXES, [((i + 1) % count, i) for i in range(count)]),
         ],
-        axis=0,
+        axis=axis,
     )
 
 
@@ -80,6 +83,111 @@
 
 def split_dot(onehot, values):
     return jnp.dot(onehot.astype(jnp.float32), values, precision=lax.Precision.HIGH)
+
+
+LANES = 128
+ROWS = 40
+
+
+def stage_tables(deriv_r, deriv_s, lift, degree):
+    basis_count = deriv_r.shape[0]
+    nodes = degree + 1
+    lift_t = jnp.zeros((ROWS, basis_count), jnp.float32).at[: 3 * nodes].set(lift.T)
+    deriv_t = jnp.zeros((144, basis_count), jnp.float32)
+    deriv_t = deriv_t.at[:basis_count].set(deriv_r.T).at[72 : 72 + basis_count].set(deriv_s.T)
+    ones_table = face_table(degree)
+    faces = ones_table.shape[0]
+    own = np.zeros((basis_count, ROWS), np.float32)
+    own[:, : faces * nodes] = ones_table.reshape(faces * nodes, basis_count).T
+    parts = [own]
+    for g in range(faces):
+        other = np.zeros((basis_count, ROWS), np.float32)
+        for f in range(faces):
+            other[:, f * nodes : (f + 1) * nodes] = -ones_table[g, ::-1, :].T
+        parts.append(other)
+    surf = jnp.asarray(np.concatenate(parts, axis=1))
+    return lift_t, deriv_t, surf
+
+
+def stage_kernel(x_ref, met_ref, geo_ref, li_ref, nf_ref, lt_ref, dt_ref, sm_ref, out_ref, s2_ref, s1_ref, z_ref):
+    fields, basis_count, width = x_ref.shape
+    blocks = width // LANES
+    z_ref[:, 0:LANES] = jnp.zeros((fields * ROWS, LANES), jnp.float32)
+    z_ref[:, width + LANES : width + 2 * LANES] = jnp.zeros((fields * ROWS, LANES), jnp.float32)
+    rowface = lax.broadcasted_iota(jnp.int32, (ROWS, LANES), 0) // (ORDER + 1)
+    window = lax.broadcasted_iota(jnp.int32, (3 * LANES, LANES), 0)
+
+    def dot(a, b):
+        return jnp.dot(a, b, precision=highest, preferred_element_type=jnp.float32)
+
+    def run(src_ref, kind):
+        def traces(b, carry):
+            off = pl.multiple_of(b * LANES, LANES)
+            lifted = [dot(lt_ref[...], src_ref[c, :, pl.ds(off, LANES)]) for c in range(fields)]
+            half_scale = geo_ref[0, :, pl.ds(off, LANES)]
+            normal_x = geo_ref[1, :, pl.ds(off, LANES)]
+            normal_y = geo_ref[2, :, pl.ds(off, LANES)]
+            height, along_x, along_y = lifted
+            face_height = half_scale * (
+                gravity * (normal_x * along_x + normal_y * along_y) - wave_speed * height
+            )
+            face_along_x = half_scale * (depth * normal_x * height - wave_speed * along_x)
+            face_along_y = half_scale * (depth * normal_y * height - wave_speed * along_y)
+            dst = pl.multiple_of(off + LANES, LANES)
+            z_ref[0:ROWS, pl.ds(dst, LANES)] = face_height
+            z_ref[ROWS : 2 * ROWS, pl.ds(dst, LANES)] = face_along_x
+            z_ref[2 * ROWS : 3 * ROWS, pl.ds(dst, LANES)] = face_along_y
+            return carry
+
+        lax.fori_loop(0, blocks, traces, 0)
+
+        def update(b, carry):
+            off = pl.multiple_of(b * LANES, LANES)
+            near = z_ref[:, pl.ds(off, 3 * LANES)]
+            gathered = []
+            for g in range(3):
+                spot = li_ref[g : g + 1, pl.ds(off, LANES)] - (off - LANES)
+                onehot = (window == spot).astype(jnp.float32)
+                across = nf_ref[g : g + 1, pl.ds(off, LANES)]
+                picked = dot(near, onehot)
+                gathered.append((picked, rowface == across))
+            m = met_ref[:, pl.ds(off, LANES)]
+            m0, m1, m2, m3 = (m[k : k + 1] for k in range(4))
+            cur = [src_ref[c, :, pl.ds(off, LANES)] for c in range(fields)]
+            rs = [dot(dt_ref[...], cur[c]) for c in range(fields)]
+            along_r = [v[0:basis_count] for v in rs]
+            along_s = [v[72 : 72 + basis_count] for v in rs]
+            volume = [
+                -gravity * (m0 * along_r[1] + m1 * along_s[1] + m2 * along_r[2] + m3 * along_s[2]),
+                -depth * (m0 * along_r[0] + m1 * along_s[0]),
+                -depth * (m2 * along_r[0] + m3 * along_s[0]),
+            ]
+            for c in range(fields):
+                own = z_ref[c * ROWS : (c + 1) * ROWS, pl.ds(pl.multiple_of(off + LANES, LANES), LANES)]
+                pieces = [own] + [
+                    jnp.where(mask, picked[c * ROWS : (c + 1) * ROWS], 0.0) for picked, mask in gathered
+                ]
+                surface = dot(sm_ref[...], jnp.concatenate(pieces, axis=0))
+                new = cur[c] + time_step * (volume[c] + surface)
+                if kind == 0:
+                    s2_ref[c, :, pl.ds(off, LANES)] = 2.0 / 3.0 * new
+                elif kind == 1:
+                    s1_ref[c, :, pl.ds(off, LANES)] = 0.25 * new
+                else:
+                    dst = pl.multiple_of(off - LANES, LANES)
+                    out_ref[c, :, pl.ds(dst, LANES)] = (
+                        x_ref[c, :, pl.ds(off, LANES)] / 3.0 + 0.75 * s2_ref[c, :, pl.ds(off, LANES)] + new
+                    )
+            return carry
+
+        if kind == 2:
+            lax.fori_loop(1, blocks - 1, update, 0)
+        else:
+            lax.fori_loop(0, blocks, update, 0)
+
+    run(x_ref, 0)
+    run(s2_ref, 1)
+    run(s1_ref, 2)
 
 
 def body(
@@ -105,61 +213,36 @@
     first_elem = lax.axis_index(AXES) * elem_count
     width = elem_count + 2 * HALO
 
-    state = adjoint.reshape(fields * basis_count, elem_count).T
-    params = jnp.concatenate([metric, face_scale, face_angle], axis=0).T
-    links = jnp.concatenate([neighbours, neighbour_face], axis=0).T
-    both = extended(jnp.concatenate([state, params], axis=1), HALO)
-    links = extended(links, HALO)
-    start = both[:, : fields * basis_count]
-    params = both[:, fields * basis_count :]
-    m0, m1, m2, m3 = (params[:, k : k + 1] for k in range(4))
-    half_scale = 0.5 * params[:, 4:7][:, :, None]
-    angle = params[:, 7:10][:, :, None]
-    normal_x = jnp.cos(angle)
-    normal_y = jnp.sin(angle)
-    local_index = (links[:, 0:3] - first_elem + HALO + elem_total) % elem_total
+    state = adjoint.reshape(fields * basis_count, elem_count)
+    params = jnp.concatenate([state, metric, face_scale, face_angle], axis=0)
+    params = extended(params, HALO, axis=1)
+    links = extended(jnp.concatenate([neighbours, neighbour_face], axis=0), HALO, axis=1)
+    start = params[: fields * basis_count].reshape(fields, basis_count, width)
+    params = params[fields * basis_count :]
+    met = params[0:4]
+    half_scale = 0.5 * params[4:7]
+    angle = params[7:10]
+
+    def spread(v):
+        rows = jnp.repeat(v, nodes, axis=0)
+        return jnp.concatenate([rows, jnp.zeros((ROWS - 3 * nodes, width), jnp.float32)], axis=0)
+
+    geo = jnp.stack([spread(half_scale), spread(jnp.cos(angle)), spread(jnp.sin(angle))])
+    local_index = (links[0:3] - first_elem + HALO + elem_total) % elem_total
     local_index = jnp.clip(local_index, 0, width - 1)
-    across_face = links[:, 3:6][:, :, None, None]
-
-    mats = jnp.concatenate([deriv_r, deriv_s, lift], axis=1)
-    surf = surface_matrix(ORDER)
-
-    def advance(current):
-        cur = current.reshape(width, fields, basis_count)
-        prod = jnp.einsum("wcp,pk->wck", cur, mats, precision=highest)
-        along_r = prod[:, :, :basis_count]
-        along_s = prod[:, :, basis_count : 2 * basis_count]
-        lifted = prod[:, :, 2 * basis_count :].reshape(width, fields, 3, nodes)
-        to_height = -gravity * (
-            m0 * along_r[:, 1] + m1 * along_s[:, 1] + m2 * along_r[:, 2] + m3 * along_s[:, 2]
-        )
-        to_along_x = -depth * (m0 * along_r[:, 0] + m1 * along_s[:, 0])
-        to_along_y = -depth * (m2 * along_r[:, 0] + m3 * along_s[:, 0])
-        height, along_x, along_y = (lifted[:, 0], lifted[:, 1], lifted[:, 2])
-        face_height = half_scale * (
-            gravity * (normal_x * along_x + normal_y * along_y) - wave_speed * height
-        )
-        face_along_x = half_scale * (depth * normal_x * height - wave_speed * along_x)
-        face_along_y = half_scale * (depth * normal_y * height - wave_speed * along_y)
-        traces = jnp.stack([face_height, face_along_x, face_along_y], axis=1)
-        rows = traces.reshape(width, fields * 3 * nodes)
-        picked = jnp.take(rows, local_index, axis=0).reshape(width, 3, fields, 3, nodes)
-        outside = jnp.where(
-            across_face == 0,
-            picked[:, :, :, 0],
-            jnp.where(across_face == 1, picked[:, :, :, 1], picked[:, :, :, 2]),
-        )
-        outside = jnp.swapaxes(outside, 1, 2).reshape(width, fields, 3 * nodes)
-        jumps = jnp.concatenate([traces.reshape(width, fields, 3 * nodes), outside], axis=2)
-        surface = jnp.einsum("wcn,np->wcp", jumps, surf, precision=highest)
-        volume = jnp.stack([to_height, to_along_x, to_along_y], axis=1)
-        return current + time_step * (volume + surface).reshape(width, fields * basis_count)
-
-    section_two = 2.0 / 3.0 * advance(start)
-    section_one = 0.25 * advance(section_two)
-    adj_rows = start / 3.0 + 0.75 * section_two + advance(section_one)
-    adj_rows = adj_rows[HALO : HALO + elem_count]
-    adj_new = adj_rows.T.reshape(fields, basis_count, elem_count)
+    across_face = links[3:6]
+    lift_t, deriv_t, surf = stage_tables(deriv_r, deriv_s, lift, ORDER)
+    adj_new = pl.pallas_call(
+        stage_kernel,
+        out_shape=jax.ShapeDtypeStruct((fields, basis_count, elem_count), jnp.float32),
+        scratch_shapes=[
+            pltpu.VMEM((fields, basis_count, width), jnp.float32),
+            pltpu.VMEM((fields, basis_count, width), jnp.float32),
+            pltpu.VMEM((fields * ROWS, width + 2 * LANES), jnp.float32),
+        ],
+        compiler_params=pltpu.CompilerParams(vmem_limit_bytes=48 * 1024 * 1024),
+    )(start, met, geo, local_index, across_face, lift_t, deriv_t, surf)
+    adj_rows = adj_new.reshape(fields * basis_count, elem_count).T
 
     rows_here = intersection_elem.shape[0]
     block_here = rows_here // BLOCK

time: 586 us -> 343 us (0.59)
  local copies, waits for them, and re-layouts: 313 us -> 86.1 us
  Pallas kernels: 0 us -> 148 us
  other arithmetic: 111 us -> 10.3 us
  matrix products: 104 us -> 41.5 us
  waiting for transfers between devices: 28.3 us -> 35.6 us
    pallas_call x0 -> x1, Pallas kernels: none -> 148 us  [body(): pl.pallas_call(stage_kernel, out_shape=jax.ShapeDtypeStruct((fields, basi...]
    gather x6 -> x0, local copies, waits for them, and re-layouts: 107 us -> none  [advance(): jnp.take(rows, local_index, axis=0).reshape(width, 3, fields, 3, nodes)]
    dot_general x6 -> x0, matrix products: 62.8 us -> none  [the longest x3 34.1 us: advance(): surface = jnp.einsum('wcn,np->wcp', jumps, surf, precision=highest)]
    select_n x3 -> x0, other arithmetic: 46.3 us -> none  [advance(): jnp.take(rows, local_index, axis=0).reshape(width, 3, fields, 3, nodes)]
    reshape x20 -> x7, local copies, waits for them, and re-layouts: 60.3 us -> 17.9 us  [the longest x2 9.28 us: body(): adj_rows = adj_new.reshape(fields * basis_count, elem_count).T]
    select_n x4 -> x0, local copies, waits for them, and re-layouts: 29.8 us -> none  [advance(): jnp.take(rows, local_index, axis=0).reshape(width, 3, fields, 3, nodes)]
    mul x9 -> x0, other arithmetic: 26 us -> none  [the longest x3 9.39 us: advance(): -gravity]
    another operation x9 -> x2, local copies, waits for them, and re-layouts: 19 us -> 0.14 us  [body(): jnp.stack([spread(half_scale), spread(jnp.cos(angle)), spread(jnp.sin(ang...]
  transfers between devices with their start and end apart: 12 -> 12, of which waited for: 5 -> 6; matrix products, arithmetic and copies ran while one was open for 3% -> 3% of each run, Pallas kernels for 0% -> 0%
where the time goes in v2:
time: 343 us; the launch traced here: 338 us
  Pallas kernels  148 us (43%)
  local copies, waits for them, and re-layouts  86.1 us (25%)
  matrix products  41.5 us (12%)
  waiting for transfers between devices  35.6 us (10%)
  starting transfers between devices  15.1 us (4%)
  other arithmetic  10.3 us (3%)
    pallas_call x1, Pallas kernels, body(): pl.pallas_call(stage_kernel, out_shape=jax.ShapeDtypeStruct((fields, basi...  148 us
    gather x2, local copies, waits for them, and re-layouts, body(): picked = jnp.take(adj_rows, intersection_elem, axis=0)  42.7 us
    ppermute x8, waiting for transfers between devices, shifted(): lax.ppermute(shard, AXES, [(i, (i + by) % length) for i in range(length)])  35.6 us
    dot_general x1, matrix products, split_dot(): jnp.dot(onehot.astype(jnp.float32), values, precision=lax.Precision.HIGH)  26 us
    dot_general x1, matrix products, body(): mapped = jnp.einsum('brci,bij->brcj', picked, chosen, precision=highest)  15.5 us
    unnamed x55, local copies, waits for them, and re-layouts  14.4 us
    ppermute x2, starting transfers between devices, extended(): lax.ppermute(head, AXES, [((i + 1) % count, i) for i in range(count)])  11.3 us
    reshape x2, local copies, waits for them, and re-layouts, body(): adj_rows = adj_new.reshape(fields * basis_count, elem_count).T  9.28 us
  transfers between devices with their start and end apart: 12, of which 6 were waited for; matrix products, arithmetic and copies ran while one was open for 3% of the time, Pallas kernels for 0%

profile of v2, /device:TPU:0, one launch (start us, length us, event | category | flops | bytes accessed | tf_op | source)
XLA Modules:
  0.0 338.3 jit_solution(5317129788437548488)
XLA Ops:
  0.7 4.2 %reshape.125 = f32[198,4096]{1,0:T(8,128)} reshape(f32[3,66,4096]{2,1,0:T(8,128)} %param.21) | data formatting | bytes 6488064 | tf_op jit(solution)/shard_map/reshape | solution.py:216
  4.9 1.0 pad_maximum_fusion.10
  5.9 0.5 collective-permute-start
  6.4 6.0 %collective-permute-start.1 = (f32[208,128]{1,0:T(8,128)S(1)}, f32[208,128]{1,0:T(8,128)S(1)}, u32[]{:S(2)}, u32[]{:S(2)}) collective-permute-start(f32[208,128]{1,0:T(8,128)S(1)} %get-tuple-element.50), channel_id=1, source_target_pairs={{1,0},{2,1},{3,2},{4,3},{5,4},{6,5},{7,6},{8,7},{9,8},{10,9},{11,1... | collective-permute-start | bytes 319496 | tf_op jit(solution)/shard_map/ppermute | solution.py:33
  12.5 5.3 %collective-permute-start.3 = (s32[6,128]{1,0:T(8,128)S(1)}, s32[6,128]{1,0:T(8,128)S(1)}, u32[]{:S(2)}, u32[]{:S(2)}) collective-permute-start(s32[6,128]{1,0:T(8,128)S(1)} %get-tuple-element.54), channel_id=1, source_target_pairs={{1,0},{2,1},{3,2},{4,3},{5,4},{6,5},{7,6},{8,7},{9,8},{10,9},{11,1... | collective-permute-start | bytes 9224 | tf_op jit(solution)/shard_map/ppermute | solution.py:33
  17.8 0.6 fusion.16
  18.5 4.6 %gather_fusion.1 = f32[64,66,66]{2,0,1:T(8,128)S(1)} fusion(f32[16,66,66]{2,0,1:T(8,128)S(1)} %copy-done, s32[1024]{0:T(1024)S(1)} %pad_clamp_fusion), kind=kCustom, calls=%fused_computation.1 | custom fusion | bytes 2230528 | tf_op jit(solution)/shard_map/jit(_take)/gather | solution.py:252
  23.1 1.6 select_bitcast_fusion
  24.7 0.1 copy.22
  24.8 0.9 copy.23
  25.7 0.7 scatter.10.lt_ref
  26.4 0.8 convert_element_type.14
  27.2 0.5 scatter.14.dt_ref
  27.9 0.5 fusion.17
  28.4 0.5 sin.3
  29.4 2.2 pad_maximum_fusion
  31.7 2.0 slice.141
  33.7 4.2 %reshape.126.x_ref = f32[3,66,4352]{2,1,0:T(8,128)} reshape(f32[198,4352]{1,0:T(8,128)} %slice.141) | data formatting | bytes 6893568 | tf_op jit(solution)/shard_map/reshape | solution.py:220
  37.9 0.1 pad_bitcast_fusion
  38.0 0.2 pad_maximum_fusion.1.geo_ref
  38.3 1.1 pad_maximum_fusion.12.met_ref
  39.4 0.7 copy-done.2
  40.1 148.2 %shard_map.158 = f32[3,66,4096]{2,1,0:T(8,128)} custom-call(f32[3,66,4352]{2,1,0:T(8,128)S(1)} %copy-done.2, f32[4,4352]{1,0:T(4,128)S(1)} %pad_maximum_fusion.12.met_ref, f32[3,40,4352]{2,1,0:T(8,128)S(1)} %pad_maximum_fusion.1.geo_ref, s32[3,4352]{1,0:T(4,128)S(1)} %get-tuple-element.52.li_ref, s32[3,4352]{1,0:T(4,128)S(1)} %get-tuple-element.51.nf_ref, ...), custom_call_target="tpu_custom_call" | custom-call | tf_op jit(solution)/shard_map/pallas_call | solution.py:235
  188.3 4.1 %reshape.130 = f32[198,4096]{1,0:T(8,128)} reshape(f32[3,66,4096]{2,1,0:T(8,128)} %shard_map.158) | data formatting | bytes 6488064 | tf_op jit(solution)/shard_map/reshape | solution.py:245
  192.4 5.2 %copy.24 = f32[198,4096]{0,1:T(8,128)} copy(f32[198,4096]{1,0:T(8,128)} %reshape.130) | data formatting | bytes 6488064 | tf_op jit(solution)/shard_map/reshape | solution.py:245
  197.6 33.5 %gather_fusion = f32[8192,198]{1,0:T(8,128)} fusion(f32[4096,198]{1,0:T(8,128)} %bitcast.29, s32[8192]{0:T(1024)S(1)} %copy-done.16), kind=kCustom, calls=%fused_computation | custom fusion | bytes 13008896 | tf_op jit(solution)/shard_map/jit(_take)/gather | solution.py:250
  231.1 9.2 %copy.25 = f32[8192,198]{0,1:T(8,128)} copy(f32[8192,198]{1,0:T(8,128)} %gather_fusion) | data formatting | bytes 12976128 | tf_op jit(solution)/shard_map/jit(_take)/gather | solution.py:250
  240.3 4.1 %copy.32 = f32[25,8,64,128]{3,2,1,0:T(8,128)S(1)} copy(f32[25,8,64,128]{3,1,2,0:T(8,128)} %bitcast.33) | data formatting | bytes 13107200
  244.4 1.2 slice.154
  245.6 1.5 broadcast_select_fusion
  247.0 0.1 copy-done.4
  247.2 15.5 %broadcast_multiply_fusion = f32[64,128,3,66]{1,3,2,0:T(8,128)S(1)} fusion(f32[64,128]{1,0:T(8,128)S(1)} %bitcast.43, f32[64,128,3,66]{1,0,3,2:T(8,128)S(1)} %broadcast_select_fusion, f32[64,66,66,1]{2,0,1,3:T(8,128)S(1)} %copy-done.4), kind=kOutput, calls=%fused_computation.19 | convolution fusion | flops 1286258688 | bytes 14124032 | tf_op jit(solution)/shard_map/brci,bij->brcj/dot_general | solution.py:253
  262.7 1.1 copy.28
  263.8 1.2 pad.74
  265.0 6.0 %copy.33 = f32[25,8,64,128]{3,1,2,0:T(8,128)S(1)} copy(f32[25,8,64,128]{3,2,1,0:T(8,128)S(1)} %bitcast.34) | data formatting | bytes 13107200
  271.0 0.1 fusion.10
  271.1 0.1 collective-permute-start.7
  271.4 1.6 collective-permute-start.5
  272.9 1.5 collective-permute-start.8
  274.4 17.4 %collective-permute-done.4 = f32[256,199]{0,1:T(8,128)S(1)} collective-permute-done((f32[256,199]{0,1:T(8,128)S(1)}, f32[256,199]{0,1:T(8,128)S(1)}, u32[]{:S(2)}, u32[]{:S(2)}) %collective-permute-start.4) | collective-permute-done | bytes 203808 | tf_op jit(solution)/shard_map/ppermute | solution.py:41
  291.9 3.4 %collective-permute-done.5 = f32[256,199]{0,1:T(8,128)S(1)} collective-permute-done((f32[256,199]{0,1:T(8,128)S(1)}, f32[256,199]{0,1:T(8,128)S(1)}, u32[]{:S(2)}, u32[]{:S(2)}) %collective-permute-start.5) | collective-permute-done | bytes 203808 | tf_op jit(solution)/shard_map/ppermute | solution.py:41
  295.3 3.5 %collective-permute-done.6 = f32[256,199]{0,1:T(8,128)S(1)} collective-permute-done((f32[256,199]{0,1:T(8,128)S(1)}, f32[256,199]{0,1:T(8,128)S(1)}, u32[]{:S(2)}, u32[]{:S(2)}) %collective-permute-start.6) | collective-permute-done | bytes 203808 | tf_op jit(solution)/shard_map/ppermute | solution.py:41
  298.9 0.4 fusion.6
  299.4 1.8 collective-permute-done.9
  301.2 5.8 %collective-permute-done.10 = f32[256,199]{0,1:T(8,128)S(1)} collective-permute-done((f32[256,199]{0,1:T(8,128)S(1)}, f32[256,199]{0,1:T(8,128)S(1)}, u32[]{:S(2)}, u32[]{:S(2)}) %collective-permute-start.10) | collective-permute-done | bytes 203808 | tf_op jit(solution)/shard_map/ppermute | solution.py:41
  307.1 3.6 %collective-permute-done.11 = f32[256,199]{0,1:T(8,128)S(1)} collective-permute-done((f32[256,199]{0,1:T(8,128)S(1)}, f32[256,199]{0,1:T(8,128)S(1)}, u32[]{:S(2)}, u32[]{:S(2)}) %collective-permute-start.11) | collective-permute-done | bytes 203808 | tf_op jit(solution)/shard_map/ppermute | solution.py:41
  310.7 26.0 %fusion = f32[198,2048]{1,0:T(8,128)S(1)} fusion(s32[8192]{0:T(1024)S(1)} %bitcast.44, f32[8192,199]{0,1:T(8,128)S(1)} %constant_dynamic-update-slice_fusion), kind=kOutput, calls=%fused_computation.3 | convolution fusion | flops 19948109824 | bytes 8175616 | tf_op jit(solution)/shard_map/dot_general | solution.py:85
  336.7 1.4 reshape.132
  (77 shorter events, 1.2 us)
Async XLA Ops:
  0.6 17.8 %copy-start = (f32[16,66,66]{2,0,1:T(8,128)S(1)}, f32[16,66,66]{2,0,1:T(8,128)}, u32[]{:S(2)}) copy-start(f32[16,66,66]{2,0,1:T(8,128)} %param.30) | copy-start | bytes 836356
  0.6 4.3 %copy-start.8 = (f32[4,4096]{1,0:T(4,128)S(1)}, f32[4,4096]{1,0:T(4,128)}, u32[]{:S(2)}) copy-start(f32[4,4096]{1,0:T(4,128)} %param.25) | copy-start | bytes 196612
  0.7 4.2 %copy-start.6 = (f32[3,4096]{1,0:T(4,128)S(1)}, f32[3,4096]{1,0:T(4,128)}, u32[]{:S(2)}) copy-start(f32[3,4096]{1,0:T(4,128)} %param.26) | copy-start | bytes 147460
  0.7 4.2 %copy-start.5 = (f32[3,4096]{1,0:T(4,128)S(1)}, f32[3,4096]{1,0:T(4,128)}, u32[]{:S(2)}) copy-start(f32[3,4096]{1,0:T(4,128)} %param.27) | copy-start | bytes 147460
  0.7 11.7 %copy-start.15 = (s32[3,4096]{1,0:T(4,128)S(1)}, s32[3,4096]{1,0:T(4,128)}, u32[]{:S(2)}) copy-start(s32[3,4096]{1,0:T(4,128)} %param.28) | copy-start | bytes 147460
  0.7 11.7 %copy-start.14 = (s32[3,4096]{1,0:T(4,128)S(1)}, s32[3,4096]{1,0:T(4,128)}, u32[]{:S(2)}) copy-start(s32[3,4096]{1,0:T(4,128)} %param.29) | copy-start | bytes 147460
  0.7 17.1 %copy-start.20 = (s32[64]{0:T(128)S(1)}, s32[64]{0:T(128)}, u32[]{:S(2)}) copy-start(s32[64]{0:T(128)} %param.34) | copy-start | bytes 772
  0.7 17.1 %copy-start.17 = (s32[8192]{0:T(1024)S(1)}, s32[8192]{0:T(1024)}, u32[]{:S(2)}) copy-start(s32[8192]{0:T(1024)} %param.31) | copy-start | bytes 98308
  5.9 22.0 %collective-permute-start = (f32[208,128]{1,0:T(8,128)S(1)}, f32[208,128]{1,0:T(8,128)S(1)}, u32[]{:S(2)}, u32[]{:S(2)}) collective-permute-start(f32[208,128]{1,0:T(8,128)S(1)} %get-tuple-element.49), channel_id=1, source_target_pairs={{0,1},{1,2},{2,3},{3,4},{4,5},{5,6},{6,7},{7,8},{8,9},{9,10},{10,1... | collective-permute-start | bytes 319496 | tf_op jit(solution)/shard_map/ppermute | solution.py:31
  6.4 21.5 %collective-permute-start.1 = (f32[208,128]{1,0:T(8,128)S(1)}, f32[208,128]{1,0:T(8,128)S(1)}, u32[]{:S(2)}, u32[]{:S(2)}) collective-permute-start(f32[208,128]{1,0:T(8,128)S(1)} %get-tuple-element.50), channel_id=1, source_target_pairs={{1,0},{2,1},{3,2},{4,3},{5,4},{6,5},{7,6},{8,7},{9,8},{10,9},{11,1... | collective-permute-start | bytes 319496 | tf_op jit(solution)/shard_map/ppermute | solution.py:33
  12.4 15.3 %collective-permute-start.2 = (s32[6,128]{1,0:T(8,128)S(1)}, s32[6,128]{1,0:T(8,128)S(1)}, u32[]{:S(2)}, u32[]{:S(2)}) collective-permute-start(s32[6,128]{1,0:T(8,128)S(1)} %get-tuple-element.53), channel_id=1, source_target_pairs={{0,1},{1,2},{2,3},{3,4},{4,5},{5,6},{6,7},{7,8},{8,9},{9,10},{10,1... | collective-permute-start | bytes 9224 | tf_op jit(solution)/shard_map/ppermute | solution.py:31
  12.5 15.2 %collective-permute-start.3 = (s32[6,128]{1,0:T(8,128)S(1)}, s32[6,128]{1,0:T(8,128)S(1)}, u32[]{:S(2)}, u32[]{:S(2)}) collective-permute-start(s32[6,128]{1,0:T(8,128)S(1)} %get-tuple-element.54), channel_id=1, source_target_pairs={{1,0},{2,1},{3,2},{4,3},{5,4},{6,5},{7,6},{8,7},{9,8},{10,9},{11,1... | collective-permute-start | bytes 9224 | tf_op jit(solution)/shard_map/ppermute | solution.py:33
  18.4 6.3 %copy-start.18 = (f32[66,66]{1,0:T(8,128)S(1)}, f32[66,66]{1,0:T(8,128)}, u32[]{:S(2)}) copy-start(f32[66,66]{1,0:T(8,128)} %param.22) | copy-start | bytes 52276
  27.7 1.7 copy-start.7
  27.7 1.7 copy-start.9
  27.8 1.4 copy-start.10
  27.9 1.3 copy-start.12
  33.7 4.5 %copy-start.11 = (f32[208,128]{1,0:T(8,128)S(1)}, f32[208,128]{1,0:T(8,128)}, u32[]{:S(2)}) copy-start(f32[208,128]{1,0:T(8,128)} %copy-done.10) | copy-start | bytes 319492
  33.7 4.5 %copy-start.13 = (f32[208,128]{1,0:T(8,128)S(1)}, f32[208,128]{1,0:T(8,128)}, u32[]{:S(2)}) copy-start(f32[208,128]{1,0:T(8,128)} %copy-done.12) | copy-start | bytes 319492
  37.9 2.1 copy-start.2
  37.9 2.1 copy-start.3
  188.3 9.3 %copy-start.16 = (s32[8192]{0:T(1024)S(1)}, s32[8192]{0:T(1024)}, u32[]{:S(2)}) copy-start(s32[8192]{0:T(1024)} %fusion.16) | copy-start | bytes 98308
  245.5 1.6 copy-start.4
  245.6 1.6 copy-start.19
  271.1 27.7 %collective-permute-start.7 = (f32[1024,199]{0,1:T(8,128)S(1)}, f32[1024,199]{0,1:T(8,128)S(1)}, u32[]{:S(2)}, u32[]{:S(2)}) collective-permute-start(f32[1024,199]{0,1:T(8,128)S(1)} %get-tuple-element.47), channel_id=1, source_target_pairs={{0,31},{1,0},{2,1},{3,2},{4,3},{5,4},{6,5},{7,6},{8,7},{9,8},{10,9... | collective-permute-start | bytes 2445320 | tf_op jit(solution)/shard_map/ppermute | solution.py:41
  271.3 20.6 %collective-permute-start.4 = (f32[256,199]{0,1:T(8,128)S(1)}, f32[256,199]{0,1:T(8,128)S(1)}, u32[]{:S(2)}, u32[]{:S(2)}) collective-permute-start(f32[256,199]{0,1:T(8,128)S(1)} %get-tuple-element.44), channel_id=1, source_target_pairs={{0,28},{1,29},{2,30},{3,31},{4,0},{5,1},{6,2},{7,3},{8,4},{9,5},{1... | collective-permute-start | bytes 611336 | tf_op jit(solution)/shard_map/ppermute | solution.py:41
  271.4 24.0 %collective-permute-start.5 = (f32[256,199]{0,1:T(8,128)S(1)}, f32[256,199]{0,1:T(8,128)S(1)}, u32[]{:S(2)}, u32[]{:S(2)}) collective-permute-start(f32[256,199]{0,1:T(8,128)S(1)} %get-tuple-element.43), channel_id=1, source_target_pairs={{0,29},{1,30},{2,31},{3,0},{4,1},{5,2},{6,3},{7,4},{8,5},{9,6},{10... | collective-permute-start | bytes 611336 | tf_op jit(solution)/shard_map/ppermute | solution.py:41
  272.9 25.9 %collective-permute-start.6 = (f32[256,199]{0,1:T(8,128)S(1)}, f32[256,199]{0,1:T(8,128)S(1)}, u32[]{:S(2)}, u32[]{:S(2)}) collective-permute-start(f32[256,199]{0,1:T(8,128)S(1)} %get-tuple-element.42), channel_id=1, source_target_pairs={{0,30},{1,31},{2,0},{3,1},{4,2},{5,3},{6,4},{7,5},{8,6},{9,7},{10,... | collective-permute-start | bytes 611336 | tf_op jit(solution)/shard_map/ppermute | solution.py:41
  272.9 26.4 %collective-permute-start.8 = (f32[1024,199]{0,1:T(8,128)S(1)}, f32[1024,199]{0,1:T(8,128)S(1)}, u32[]{:S(2)}, u32[]{:S(2)}) collective-permute-start(f32[1024,199]{0,1:T(8,128)S(1)} %get-tuple-element.46), channel_id=1, source_target_pairs={{0,1},{1,2},{2,3},{3,4},{4,5},{5,6},{6,7},{7,8},{8,9},{9,10},{10,1... | collective-permute-start | bytes 2445320 | tf_op jit(solution)/shard_map/ppermute | solution.py:41
  291.9 9.4 %collective-permute-start.9 = (f32[256,199]{0,1:T(8,128)S(1)}, f32[256,199]{0,1:T(8,128)S(1)}, u32[]{:S(2)}, u32[]{:S(2)}) collective-permute-start(f32[256,199]{0,1:T(8,128)S(1)} %get-tuple-element.41), channel_id=1, source_target_pairs={{0,2},{1,3},{2,4},{3,5},{4,6},{5,7},{6,8},{7,9},{8,10},{9,11},{10,... | collective-permute-start | bytes 611336 | tf_op jit(solution)/shard_map/ppermute | solution.py:41
  295.3 11.7 %collective-permute-start.10 = (f32[256,199]{0,1:T(8,128)S(1)}, f32[256,199]{0,1:T(8,128)S(1)}, u32[]{:S(2)}, u32[]{:S(2)}) collective-permute-start(f32[256,199]{0,1:T(8,128)S(1)} %get-tuple-element.45), channel_id=1, source_target_pairs={{0,3},{1,4},{2,5},{3,6},{4,7},{5,8},{6,9},{7,10},{8,11},{9,12},{10... | collective-permute-start | bytes 611336 | tf_op jit(solution)/shard_map/ppermute | solution.py:41
  298.8 11.8 %collective-permute-start.11 = (f32[256,199]{0,1:T(8,128)S(1)}, f32[256,199]{0,1:T(8,128)S(1)}, u32[]{:S(2)}, u32[]{:S(2)}) collective-permute-start(f32[256,199]{0,1:T(8,128)S(1)} %get-tuple-element.40), channel_id=1, source_target_pairs={{0,4},{1,5},{2,6},{3,7},{4,8},{5,9},{6,10},{7,11},{8,12},{9,13},{1... | collective-permute-start | bytes 611336 | tf_op jit(solution)/shard_map/ppermute | solution.py:41
  310.7 27.4 %copy-start.1 = (f32[16,66,66]{2,0,1:T(8,128)S(1)}, f32[16,66,66]{2,0,1:T(8,128)}, u32[]{:S(2)}) copy-start(f32[16,66,66]{2,0,1:T(8,128)} %param.30) | copy-start | bytes 836356
